TPU v7x, 512 devices: a whole 4x4x16 slice. The times are simulated.
512 devices in a mesh: ctx: 64 (over z, y), head: 8 (over x, core).
Axes of the slice: x: 4, y: 4, z: 16, core: 2. Of those that a mesh axis runs over, the one named last changes fastest.
Arguments:
- queries: bfloat16 [8192, 4096], P(('ctx', 'head')), may hold values from -4.6 to 4.6
- key_states: bfloat16 [8192, 4096], P(('ctx', 'head')), may hold values from -4.6 to 4.6
- value_states: bfloat16 [8192, 4096], P(('ctx', 'head')), may hold values from -6 to 6
- out_grad: bfloat16 [8192, 4096], P(('ctx', 'head')), may hold values from -6 to 6
- random_blocks: int32 [256, 3], replicated, may hold values from 0 to 255, as said below
- global_blocks: int32 [4], replicated, may hold values from 0 to 255, as said below
Outputs:
- query_grad: bfloat16 [8192, 4096], P('ctx', 'head')
- key_grad: bfloat16 [8192, 4096], P('ctx', 'head')
- value_grad: bfloat16 [8192, 4096], P('ctx', 'head')
Inputs may be any that keep to these rules, and one draw needn't show every extreme that they name: `random_blocks`: with the blocks i * 4 to i * 4 + 3 called range i: the 12 entries of the rows of range i name blocks of any one range at most 1 times, and some range exactly 1 times. `global_blocks`: 4 different blocks, one of them the last block 255, in any order.
All inputs are finite; a program needn't handle non-finite values.
Results may differ from a plain program's by a relative error of at most 0.0077.
Values may be sent and summed in bfloat16 or wider, within the bound.
No kernel may reach another device: no remote copies, remote signals or barrier semaphores. Data moves between devices by JAX's collectives and lax.ppermute only.
A program may use at most 128 MiB of HBM per device.

v0:
```python
import math

import jax
import jax.numpy as jnp
from jax import lax
from jax.sharding import PartitionSpec as P

DH = 128
BS = 32
NR = 3
NG = 4


def with_halo(x, sides, width):
    for axis, dim in sides:
        peers, length = (lax.axis_size(axis), x.shape[dim])
        up = [(i, (i + 1) % peers) for i in range(peers - 1)]
        down = [(j, i) for i, j in up]
        last = lax.slice_in_dim(x, length - width, length, axis=dim)
        first = lax.slice_in_dim(x, 0, width, axis=dim)
        before = lax.ppermute(last, axis, up)
        after = lax.ppermute(first, axis, down)
        x = jnp.concatenate([before, x, after], axis=dim)
    return x


def spread(x, axis, root):
    mine = lax.axis_index(axis) == root
    return lax.psum(jnp.where(mine, x, jnp.zeros_like(x)), axis)


def per_device(queries, key_states, value_states, out_grad, random_blocks, global_blocks):
    query_rows, key_rows, value_rows, grad_rows = (
        lax.all_to_all(queries, "head", split_axis=1, concat_axis=0, tiled=True),
        lax.all_to_all(key_states, "head", split_axis=1, concat_axis=0, tiled=True),
        lax.all_to_all(value_states, "head", split_axis=1, concat_axis=0, tiled=True),
        lax.all_to_all(out_grad, "head", split_axis=1, concat_axis=0, tiled=True),
    )
    tokens = query_rows.shape[0]
    head_cols = query_rows.shape[1]
    heads_here = head_cols // DH
    blocks_here = tokens // BS
    devices = lax.axis_size("ctx")
    my_index = lax.axis_index("ctx")
    total_blocks = devices * blocks_here
    entries = blocks_here * NR
    capacity = (entries + devices - 1) // devices
    inv_root = 1.0 / math.sqrt(DH)
    kv_rows = jnp.concatenate([key_rows, value_rows], axis=1)
    kv_blocks = kv_rows.reshape(blocks_here, BS, 2 * head_cols)
    extended = with_halo(kv_rows, (("ctx", 0),), BS)
    extended = extended.reshape(blocks_here + 2, BS, 2 * head_cols)
    window = jnp.stack(
        [extended[:blocks_here], extended[1 : blocks_here + 1], extended[2:]], axis=1
    )
    global_owner = global_blocks // blocks_here
    global_offset = global_blocks % blocks_here
    pieces = []
    for member in range(NG):
        own_block = lax.dynamic_index_in_dim(kv_blocks, global_offset[member], 0, keepdims=False)
        pieces.append(spread(own_block, "ctx", global_owner[member]))
    global_kv = jnp.stack(pieces)
    entry_table = random_blocks.reshape(devices, entries)
    table_owner = entry_table // blocks_here
    table_offset = entry_table % blocks_here
    positions = jnp.arange(entries, dtype=jnp.int32)
    before = positions[None, :] < positions[:, None]
    matches = (table_owner[:, :, None] == table_owner[:, None, :]) & before[None]
    table_slot = jnp.sum(matches.astype(jnp.int32), axis=2)
    my_owner = lax.dynamic_index_in_dim(table_owner, my_index, 0, keepdims=False)
    my_slot = lax.dynamic_index_in_dim(table_slot, my_index, 0, keepdims=False)
    my_target = my_owner * capacity + my_slot
    slot_ids = jnp.arange(capacity, dtype=jnp.int32)
    served = (table_owner == my_index)[:, :, None] & (
        table_slot[:, :, None] == slot_ids[None, None, :]
    )
    served_block = jnp.sum(jnp.where(served, table_offset[:, :, None], 0), axis=1).reshape(-1)
    served_used = jnp.any(served, axis=1).reshape(-1)
    outgoing = jnp.take(kv_blocks, served_block, axis=0)
    incoming = lax.all_to_all(outgoing, "ctx", split_axis=0, concat_axis=0, tiled=True)
    fetched = jnp.take(incoming, my_target, axis=0).reshape(blocks_here, NR, BS, 2 * head_cols)
    near_kv = jnp.concatenate([window, fetched], axis=1)
    near_groups = 3 + NR
    near_count = near_groups * BS
    query_heads = query_rows.reshape(blocks_here, BS, heads_here, DH)
    grad_heads = grad_rows.reshape(blocks_here, BS, heads_here, DH)
    near_keys = near_kv[..., :head_cols].reshape(blocks_here, near_groups, BS, heads_here, DH)
    near_values = near_kv[..., head_cols:].reshape(blocks_here, near_groups, BS, heads_here, DH)
    far_keys = global_kv[..., :head_cols].reshape(NG, BS, heads_here, DH)
    far_values = global_kv[..., head_cols:].reshape(NG, BS, heads_here, DH)
    scores = (
        jnp.concatenate(
            [
                jnp.einsum(
                    "bqhd,bgkhd->bhqgk", query_heads, near_keys, preferred_element_type=jnp.float32
                ).reshape(blocks_here, heads_here, BS, near_count),
                jnp.einsum(
                    "bqhd,gkhd->bhqgk", query_heads, far_keys, preferred_element_type=jnp.float32
                ).reshape(blocks_here, heads_here, BS, NG * BS),
            ],
            axis=3,
        )
        * inv_root
    )
    block_ids = my_index * blocks_here + jnp.arange(blocks_here, dtype=jnp.int32)
    usable = jnp.concatenate(
        [
            (block_ids > 0)[:, None],
            jnp.ones((blocks_here, 1), bool),
            (block_ids < total_blocks - 1)[:, None],
            jnp.ones((blocks_here, NR + NG), bool),
        ],
        axis=1,
    )
    column_ok = jnp.repeat(usable, BS, axis=1)[:, None, None, :]
    masked = jnp.where(column_ok, scores, -jnp.inf)
    row_max = jnp.max(masked, axis=3, keepdims=True)
    log_total = row_max + jnp.log(jnp.sum(jnp.exp(masked - row_max), axis=3, keepdims=True))
    probs_full = jnp.exp(masked - log_total)
    probs_half = probs_full.astype(jnp.bfloat16)
    near_probs = probs_half[..., :near_count].reshape(blocks_here, heads_here, BS, near_groups, BS)
    far_probs = probs_half[..., near_count:].reshape(blocks_here, heads_here, BS, NG, BS)
    outputs = jnp.einsum(
        "bhqgk,bgkhd->bqhd", near_probs, near_values, preferred_element_type=jnp.float32
    ) + jnp.einsum("bhqgk,gkhd->bqhd", far_probs, far_values, preferred_element_type=jnp.float32)
    row_dot = jnp.sum(grad_heads.astype(jnp.float32) * outputs, axis=3)
    dprobs = jnp.concatenate(
        [
            jnp.einsum(
                "bqhd,bgkhd->bhqgk", grad_heads, near_values, preferred_element_type=jnp.float32
            ).reshape(blocks_here, heads_here, BS, near_count),
            jnp.einsum(
                "bqhd,gkhd->bhqgk", grad_heads, far_values, preferred_element_type=jnp.float32
            ).reshape(blocks_here, heads_here, BS, NG * BS),
        ],
        axis=3,
    )
    dscores = probs_full * (dprobs - jnp.transpose(row_dot, (0, 2, 1))[..., None])
    ds_half = dscores.astype(jnp.bfloat16)
    near_ds = ds_half[..., :near_count].reshape(blocks_here, heads_here, BS, near_groups, BS)
    far_ds = ds_half[..., near_count:].reshape(blocks_here, heads_here, BS, NG, BS)
    query_grad = (
        (
            (
                jnp.einsum(
                    "bhqgk,bgkhd->bqhd", near_ds, near_keys, preferred_element_type=jnp.float32
                )
                + jnp.einsum(
                    "bhqgk,gkhd->bqhd", far_ds, far_keys, preferred_element_type=jnp.float32
                )
            )
            * inv_root
        )
        .astype(jnp.bfloat16)
        .reshape(tokens, head_cols)
    )

    def key_value_parts(ds_part, probs_part):
        key_part = (
            jnp.einsum(
                "bhqgk,bqhd->bgkhd", ds_part, query_heads, preferred_element_type=jnp.float32
            )
            * inv_root
        )
        value_part = jnp.einsum(
            "bhqgk,bqhd->bgkhd", probs_part, grad_heads, preferred_element_type=jnp.float32
        )
        out_shape = key_part.shape[:3] + (head_cols,)
        return jnp.concatenate([key_part.reshape(out_shape), value_part.reshape(out_shape)], axis=3)

    random_part = key_value_parts(near_ds[:, :, :, 3:], near_probs[:, :, :, 3:])
    random_part = random_part.astype(jnp.bfloat16).reshape(entries, BS, 2 * head_cols)
    back_rows = (
        jnp.zeros((devices * capacity, BS, 2 * head_cols), jnp.bfloat16)
        .at[my_target]
        .set(random_part)
    )
    arrived = lax.all_to_all(back_rows, "ctx", split_axis=0, concat_axis=0, tiled=True)
    window_part = key_value_parts(near_ds[:, :, :, :3], near_probs[:, :, :, :3])
    zero_block = jnp.zeros((1, BS, 2 * head_cols), jnp.float32)
    own_grad = (
        window_part[:, 1]
        + jnp.concatenate([window_part[1:, 0], zero_block], axis=0)
        + jnp.concatenate([zero_block, window_part[:-1, 2]], axis=0)
    )
    rims_out = jnp.concatenate([window_part[0, 0], window_part[blocks_here - 1, 2]], axis=0)
    rims_in = with_halo(rims_out.astype(jnp.bfloat16), (("ctx", 0),), BS).astype(rims_out.dtype)
    own_grad = own_grad.at[0].add(rims_in[:BS]).at[blocks_here - 1].add(rims_in[3 * BS :])
    far_key = (
        jnp.einsum("bhqgk,bqhd->gkhd", far_ds, query_heads, preferred_element_type=jnp.float32)
        * inv_root
    )
    far_value = jnp.einsum(
        "bhqgk,bqhd->gkhd", far_probs, grad_heads, preferred_element_type=jnp.float32
    )
    far_part = jnp.concatenate(
        [far_key.reshape(NG, BS, head_cols), far_value.reshape(NG, BS, head_cols)], axis=2
    )
    far_sum = lax.psum(far_part, "ctx")
    here_ids = jnp.arange(blocks_here, dtype=jnp.int32)
    own_global = (
        (global_owner == my_index)[None, :] & (global_offset[None, :] == here_ids[:, None])
    ).astype(jnp.float32)
    own_grad = own_grad + jnp.einsum(
        "jg,gkc->jkc", own_global, far_sum, precision=lax.Precision.HIGHEST
    )
    weights = (served_used[None, :] & (served_block[None, :] == here_ids[:, None])).astype(
        jnp.bfloat16
    )
    own_grad = own_grad + jnp.einsum(
        "jr,rkc->jkc", weights, arrived, preferred_element_type=jnp.float32
    )
    key_grad = own_grad[..., :head_cols].astype(jnp.bfloat16).reshape(tokens, head_cols)
    value_grad = own_grad[..., head_cols:].astype(jnp.bfloat16).reshape(tokens, head_cols)
    return (query_grad, key_grad, value_grad)


def solution(mesh):
    placed = (
        P(("ctx", "head"), None),
        P(("ctx", "head"), None),
        P(("ctx", "head"), None),
        P(("ctx", "head"), None),
        P(),
        P(),
    )
    return jax.shard_map(
        per_device,
        mesh=mesh,
        in_specs=placed,
        out_specs=(P("ctx", "head"), P("ctx", "head"), P("ctx", "head")),
        check_vma=False,
    )
```

profile of v0, /device:TPU:6, one launch (start us, length us, event | category | flops | bytes accessed | tf_op | source)
XLA Modules:
  0.0 762.6 jit_solution(3867168004326014338)
XLA Ops:
  7.2 1.6 copy.526
  8.8 9.2 %all-to-all-start = ((bf16[16,8,512]{2,0,1:T(8,128)(2,1)}), bf16[16,8,512]{2,0,1:T(8,128)(2,1)S(1)}, u32[]{:S(2)}, u32[]{:S(2)}) async-start(bf16[16,8,512]{2,0,1:T(8,128)(2,1)} %bitcast.216), calls=%async_computation | async-start | bytes 262144 | tf_op jit(solution)/shard_map/all_to_all | solution.py:35
  18.0 0.7 broadcast_compare_fusion.1
  18.7 0.8 copy.297
  20.2 0.8 fusion.90
  21.3 0.7 copy.525
  22.1 5.3 all-to-all-start.1
  27.4 0.7 copy.524
  28.1 0.7 copy.523
  28.8 2.7 all-to-all-done.1
  31.4 5.4 all-to-all-start.3
  36.9 2.8 gather_fusion
  39.7 1.2 all-to-all-done.3
  40.9 5.4 all-to-all-start.4
  46.3 4.6 broadcast_select_fusion
  50.9 14.8 %all-to-all-start.2 = ((bf16[64,32,1024]{2,1,0:T(8,128)(2,1)}), bf16[64,32,1024]{2,1,0:T(8,128)(2,1)}, u32[]{:S(2)}, u32[]{:S(2)}) async-start(bf16[64,32,1024]{2,1,0:T(8,128)(2,1)} %broadcast_select_fusion), calls=%async_computation.2 | async-start | bytes 8388608 | tf_op jit(solution)/shard_map/all_to_all | solution.py:80
  65.8 0.6 fusion.96
  71.6 0.5 broadcast_compare_fusion.2
  72.2 0.7 fusion.95
  78.5 0.6 compare_and_fusion.1
  79.1 0.7 fusion.72
  80.0 3.4 collective-permute-start
  83.4 1.5 collective-permute-start.1
  84.8 0.7 maximum_bitcast_fusion
  85.6 4.0 collective-permute-done.1
  89.6 0.8 pad_maximum_fusion.6
  90.4 298.1 %all-reduce.8.cloned.1.call-done = (bf16[1,32,1024]{2,1,0:T(8,128)(2,1)}, bf16[1,32,1024]{2,1,0:T(8,128)(2,1)}, bf16[1,32,1024]{2,1,0:T(8,128)(2,1)}, bf16[1,32,1024]{2,1,0:T(8,128)(2,1)}) async-done(((bf16[1,32,1024]{2,1,0:T(8,128)(2,1)}, bf16[1,32,1024]{2,1,0:T(8,128)(2,1)}, bf16[1,32,1024]{2,1,0:T(8,128)(2,1)}, bf16[1,32,1024]{2,1,0:T(8,128)(2,1)}), (bf16[1,32,1024]{2,1,0:T(8,128)(2,1)}, ...) | async-done | bytes 262160 | tf_op jit(solution)/shard_map/psum | solution.py:29
  388.5 0.8 constant_dynamic-update-slice_fusion.3
  389.3 0.8 constant_dynamic-update-slice_fusion.2
  390.2 0.8 constant_dynamic-update-slice_fusion.1
  391.0 0.8 constant_dynamic-update-slice_fusion
  391.9 0.8 slice_bitcast_fusion.8
  394.7 1.2 reshape.369
  395.9 2.8 gather_fusion.1
  399.1 1.3 slice_bitcast_fusion.1
  400.8 0.6 copy.319
  402.7 1.0 reshape.371
  404.3 1.2 fusion.92
  405.8 0.7 copy-done.5
  406.8 1.2 fusion.15
  408.5 0.9 concatenate.86
  409.4 0.6 copy.326
  410.0 1.5 fusion.24
  412.0 1.3 fusion.93
  414.5 2.5 broadcast_in_dim.69
  417.0 2.8 scatter_fusion
  419.8 9.0 %all-to-all-start.5 = ((bf16[64,32,1024]{2,1,0:T(8,128)(2,1)}), bf16[64,32,1024]{2,1,0:T(8,128)(2,1)}, u32[]{:S(2)}, u32[]{:S(2)}) async-start(bf16[64,32,1024]{2,1,0:T(8,128)(2,1)} %scatter_fusion), calls=%async_computation.5 | async-start | bytes 8388608 | tf_op jit(solution)/shard_map/all_to_all | solution.py:178
  429.4 1.7 slice.201
  431.6 0.8 reshape.436
  432.8 0.5 copy.400
  434.4 0.9 reshape.435
  435.3 1.9 pad_maximum_fusion.2
  437.5 0.5 copy.397
  438.7 3.5 collective-permute-start.2
  442.2 1.3 collective-permute-start.3
  444.6 0.7 copy.522
  445.2 3.3 collective-permute-done.3
  449.2 1.1 scatter-add.9
  450.3 164.0 %all-to-all-done.5 = bf16[64,32,1024]{2,1,0:T(8,128)(2,1)} async-done(((bf16[64,32,1024]{2,1,0:T(8,128)(2,1)}), bf16[64,32,1024]{2,1,0:T(8,128)(2,1)}, u32[]{:S(2)}, u32[]{:S(2)}) %all-to-all-start.5) | async-done | bytes 4194336 | tf_op jit(solution)/shard_map/all_to_all | solution.py:178
  614.3 6.7 fusion
  621.0 131.6 %all-reduce.6.cloned.1.call-done = f32[4,32,1024]{2,0,1:T(4,128)} async-done(((f32[4,32,1024]{2,0,1:T(4,128)}), f32[4,32,1024]{2,0,1:T(4,128)}) %all-reduce.6.cloned.1.call-update) | async-done | bytes 524304 | tf_op jit(solution)/shard_map/psum | solution.py:199
  752.6 1.7 fusion.5
  754.4 0.7 copy.364
  755.1 0.7 copy.363
  (154 shorter events, 14.2 us)
Async XLA Ops:
  7.2 14.1 %copy-start.19 = (bf16[16,4096]{1,0:T(8,128)(2,1)S(1)}, bf16[16,4096]{1,0:T(8,128)(2,1)}, u32[]{:S(2)}) copy-start(bf16[16,4096]{1,0:T(8,128)(2,1)} %param.12) | copy-start | bytes 393220
  7.2 20.2 %copy-start.20 = (bf16[16,4096]{1,0:T(8,128)(2,1)S(1)}, bf16[16,4096]{1,0:T(8,128)(2,1)}, u32[]{:S(2)}) copy-start(bf16[16,4096]{1,0:T(8,128)(2,1)} %param.10) | copy-start | bytes 393220
  7.2 20.9 %copy-start.21 = (bf16[16,4096]{1,0:T(8,128)(2,1)S(1)}, bf16[16,4096]{1,0:T(8,128)(2,1)}, u32[]{:S(2)}) copy-start(bf16[16,4096]{1,0:T(8,128)(2,1)} %param.13) | copy-start | bytes 393220
  8.8 13.3 %all-to-all-start = ((bf16[16,8,512]{2,0,1:T(8,128)(2,1)}), bf16[16,8,512]{2,0,1:T(8,128)(2,1)S(1)}, u32[]{:S(2)}, u32[]{:S(2)}) async-start(bf16[16,8,512]{2,0,1:T(8,128)(2,1)} %bitcast.216), calls=%async_computation | async-start | bytes 262144 | tf_op jit(solution)/shard_map/all_to_all | solution.py:35
  22.1 14.8 %copy-start.23 = (s32[64]{0:T(128)}, s32[64]{0:T(128)S(1)}, u32[]{:S(2)}) copy-start(s32[64]{0:T(128)S(1)} %reduce_sum.48) | copy-start | bytes 772
  22.1 9.3 %all-to-all-start.1 = ((bf16[16,8,512]{2,0,1:T(8,128)(2,1)}), bf16[16,8,512]{2,0,1:T(8,128)(2,1)S(1)}, u32[]{:S(2)}, u32[]{:S(2)}) async-start(bf16[16,8,512]{2,0,1:T(8,128)(2,1)} %bitcast.215), calls=%async_computation.1 | async-start | bytes 262144 | tf_op jit(solution)/shard_map/all_to_all | solution.py:36
  31.4 9.4 %all-to-all-start.3 = ((bf16[16,8,512]{2,0,1:T(8,128)(2,1)}), bf16[16,8,512]{2,0,1:T(8,128)(2,1)S(1)}, u32[]{:S(2)}, u32[]{:S(2)}) async-start(bf16[16,8,512]{2,0,1:T(8,128)(2,1)} %bitcast.214), calls=%async_computation.3 | async-start | bytes 262144 | tf_op jit(solution)/shard_map/all_to_all | solution.py:34
  40.9 10.0 %all-to-all-start.4 = ((bf16[16,8,512]{2,0,1:T(8,128)(2,1)}), bf16[16,8,512]{2,0,1:T(8,128)(2,1)S(1)}, u32[]{:S(2)}, u32[]{:S(2)}) async-start(bf16[16,8,512]{2,0,1:T(8,128)(2,1)} %bitcast.213), calls=%async_computation.4 | async-start | bytes 262144 | tf_op jit(solution)/shard_map/all_to_all | solution.py:37
  50.9 14.8 %copy-start.30 = (s32[4]{0:T(128)S(1)}, s32[4]{0:T(128)}, u32[]{:S(2)}) copy-start(s32[4]{0:T(128)} %param.15) | copy-start | bytes 52
  50.9 345.0 %all-to-all-start.2 = ((bf16[64,32,1024]{2,1,0:T(8,128)(2,1)}), bf16[64,32,1024]{2,1,0:T(8,128)(2,1)}, u32[]{:S(2)}, u32[]{:S(2)}) async-start(bf16[64,32,1024]{2,1,0:T(8,128)(2,1)} %broadcast_select_fusion), calls=%async_computation.2 | async-start | bytes 8388608 | tf_op jit(solution)/shard_map/all_to_all | solution.py:80
  65.7 322.8 %all-reduce.8.cloned.1.call-start = ((), (), s32[]{:S(2)}) async-start(), calls=%async_computation.7 | async-start | bytes 524288 | tf_op jit(solution)/shard_map/psum | solution.py:29
  78.5 11.9 %copy-start.26 = (s32[12]{0:T(128)}, s32[12]{0:T(128)S(1)}, u32[]{:S(2)}) copy-start(s32[12]{0:T(128)S(1)} %fusion.89) | copy-start | bytes 148
  79.9 320.6 %copy-start.3 = (bf16[4,32,4,128]{3,2,1,0:T(4,128)(2,1)}, bf16[4,32,4,128]{3,2,1,0:T(4,128)(2,1)S(1)}, u32[]{:S(2)}) copy-start(bf16[4,32,4,128]{3,2,1,0:T(4,128)(2,1)S(1)} %reshape.361) | copy-start | bytes 393220
  80.0 5.6 collective-permute-start
  83.4 6.3 collective-permute-start.1
  394.7 4.0 copy-start.28
  395.9 3.0 copy-start.13
  395.9 3.0 copy-start.14
  400.5 0.9 copy-start
  404.3 1.2 copy-start.2
  405.5 1.0 copy-start.5
  405.5 1.1 copy-start.18
  408.5 1.5 copy-start.22
  411.5 1.9 copy-start.12
  411.5 1.9 copy-start.4
  413.4 1.0 copy-start.11
  414.4 2.6 copy-start.27
  419.8 9.3 %copy-start.25 = (pred[256]{0:T(512)(128)(4,1)S(1)}, pred[256]{0:T(512)(128)(4,1)}, u32[]{:S(2)}) copy-start(pred[256]{0:T(512)(128)(4,1)} %get-tuple-element.33) | copy-start | bytes 772
  419.8 11.3 %copy-start.6 = (bf16[4,4,32,4,32]{4,3,2,1,0:T(4,128)(2,1)S(1)}, bf16[4,4,32,4,32]{4,3,2,1,0:T(4,128)(2,1)}, u32[]{:S(2)}) copy-start(bf16[4,4,32,4,32]{4,3,2,1,0:T(4,128)(2,1)} %reshape.371) | copy-start | bytes 393220
  419.8 194.5 %all-to-all-start.5 = ((bf16[64,32,1024]{2,1,0:T(8,128)(2,1)}), bf16[64,32,1024]{2,1,0:T(8,128)(2,1)}, u32[]{:S(2)}, u32[]{:S(2)}) async-start(bf16[64,32,1024]{2,1,0:T(8,128)(2,1)} %scatter_fusion), calls=%async_computation.5 | async-start | bytes 8388608 | tf_op jit(solution)/shard_map/all_to_all | solution.py:178
  428.9 3.6 copy-start.9
  428.9 323.7 %all-reduce.6.cloned.1.call-start = ((), (), s32[]{:S(2)}) async-start(), calls=%async_computation.6 | async-start | bytes 1048576 | tf_op jit(solution)/shard_map/psum | solution.py:199
  432.8 0.9 copy-start.16
  433.7 1.6 copy-start.15
  433.9 3.2 copy-start.7
  434.2 3.0 copy-start.10
  438.5 5.0 copy-start.8
  438.5 5.0 copy-start.17
  438.6 5.3 copy-start.1
  438.7 6.6 collective-permute-start.2
  442.2 6.4 collective-permute-start.3
  444.6 169.7 %copy-start.24 = (s32[64]{0:T(128)S(1)}, s32[64]{0:T(128)}, u32[]{:S(2)}) copy-start(s32[64]{0:T(128)} %copy-done.23) | copy-start | bytes 772
  450.3 302.4 %copy-start.29 = (pred[4]{0:T(512)(128)(4,1)S(1)}, pred[4]{0:T(512)(128)(4,1)}, u32[]{:S(2)}) copy-start(pred[4]{0:T(512)(128)(4,1)} %get-tuple-element.31) | copy-start | bytes 16
Sparse Core Ops, SparseCore 0:
  80.0 308.4 all-reduce.7
  437.3 315.2 all-reduce.5
where the time goes:
time: 764 us; the launch traced here: 763 us
  waiting for transfers between devices  605 us (79%)
  starting transfers between devices  59 us (8%)
  local copies, waits for them, and re-layouts  43.9 us (6%)
  between operations  25.1 us (3%)
  other arithmetic  15.6 us (2%)
  matrix products  13.9 us (2%)
    psum x1, waiting for transfers between devices, spread(): return lax.psum(jnp.where(mine, x, jnp.zeros_like(x)), axis)  298 us
    all_to_all x1, waiting for transfers between devices, per_device(): lax.all_to_all(back_rows, 'ctx', split_axis=0, concat_axis=0, tiled=True)  164 us
    psum x1, waiting for transfers between devices, per_device(): far_sum = lax.psum(far_part, 'ctx')  132 us
  transfers between devices with their start and end apart: 12, of which 7 were waited for; matrix products, arithmetic and copies ran while one was open for 6% of the time, Pallas kernels for 0%

commit v1 on v0

--- a/solution.py
+++ b/solution.py
@@ -24,18 +24,29 @@
     return x
 
 
-def spread(x, axis, root):
-    mine = lax.axis_index(axis) == root
-    return lax.psum(jnp.where(mine, x, jnp.zeros_like(x)), axis)
+def chunk_sum(x, axis):
+    peers = lax.axis_size(axis)
+    parts = lax.all_to_all(x.reshape(peers, -1), axis, split_axis=0, concat_axis=0, tiled=True)
+    return jnp.sum(parts.astype(jnp.float32), axis=0)
+
+
+def chunk_share(chunk, axis, shape, dtype):
+    peers = lax.axis_size(axis)
+    copies = jnp.broadcast_to(chunk.astype(dtype)[None], (peers,) + chunk.shape)
+    return lax.all_to_all(copies, axis, split_axis=0, concat_axis=0, tiled=True).reshape(shape)
+
+
+def all_sum(x, axis):
+    return chunk_share(chunk_sum(x, axis), axis, x.shape, x.dtype)
 
 
 def per_device(queries, key_states, value_states, out_grad, random_blocks, global_blocks):
-    query_rows, key_rows, value_rows, grad_rows = (
-        lax.all_to_all(queries, "head", split_axis=1, concat_axis=0, tiled=True),
-        lax.all_to_all(key_states, "head", split_axis=1, concat_axis=0, tiled=True),
-        lax.all_to_all(value_states, "head", split_axis=1, concat_axis=0, tiled=True),
-        lax.all_to_all(out_grad, "head", split_axis=1, concat_axis=0, tiled=True),
-    )
+    groups = lax.axis_size("head")
+    rows_in, cols_in = queries.shape
+    stacked = jnp.stack([queries, key_states, value_states, out_grad], axis=1)
+    stacked = stacked.reshape(rows_in, 4, groups, cols_in // groups)
+    stacked = lax.all_to_all(stacked, "head", split_axis=2, concat_axis=0, tiled=True)
+    query_rows, key_rows, value_rows, grad_rows = (stacked[:, i, 0] for i in range(4))
     tokens = query_rows.shape[0]
     head_cols = query_rows.shape[1]
     heads_here = head_cols // DH
@@ -55,11 +66,9 @@
     )
     global_owner = global_blocks // blocks_here
     global_offset = global_blocks % blocks_here
-    pieces = []
-    for member in range(NG):
-        own_block = lax.dynamic_index_in_dim(kv_blocks, global_offset[member], 0, keepdims=False)
-        pieces.append(spread(own_block, "ctx", global_owner[member]))
-    global_kv = jnp.stack(pieces)
+    owned = jnp.take(kv_blocks, global_offset, axis=0)
+    owned = jnp.where((global_owner == my_index)[:, None, None], owned, jnp.zeros_like(owned))
+    global_kv = all_sum(owned, "ctx")
     entry_table = random_blocks.reshape(devices, entries)
     table_owner = entry_table // blocks_here
     table_offset = entry_table % blocks_here
@@ -196,7 +205,7 @@
     far_part = jnp.concatenate(
         [far_key.reshape(NG, BS, head_cols), far_value.reshape(NG, BS, head_cols)], axis=2
     )
-    far_sum = lax.psum(far_part, "ctx")
+    far_sum = all_sum(far_part, "ctx")
     here_ids = jnp.arange(blocks_here, dtype=jnp.int32)
     own_global = (
         (global_owner == my_index)[None, :] & (global_offset[None, :] == here_ids[:, None])

time: 764 us -> 610 us (0.80)
  the two profiles are of different devices: /device:TPU:6 before, /device:TPU:24 now
where the time goes in v1:
time: 610 us; the launch traced here: 601 us
  waiting for transfers between devices  410 us (67%)
  starting transfers between devices  59.5 us (10%)
  local copies, waits for them, and re-layouts  51.1 us (8%)
  blocking collectives  44.3 us (7%)
  other arithmetic  18.2 us (3%)
  matrix products  15.7 us (3%)
    ppermute x2, waiting for transfers between devices, with_halo(): before = lax.ppermute(last, axis, up)  334 us
    all_to_all x1, blocking collectives, chunk_sum(): lax.all_to_all(x.reshape(peers, -1), axis, split_axis=0, concat_axis=0, t...  44.3 us
    all_to_all x2, waiting for transfers between devices, chunk_share(): lax.all_to_all(copies, axis, split_axis=0, concat_axis=0, tiled=True)  31.6 us
    all_to_all x1, waiting for transfers between devices, chunk_sum(): lax.all_to_all(x.reshape(peers, -1), axis, split_axis=0, concat_axis=0, t...  20.1 us
    all_to_all x1, starting transfers between devices, chunk_sum(): lax.all_to_all(x.reshape(peers, -1), axis, split_axis=0, concat_axis=0, t...  18.5 us
    unnamed x61, local copies, waits for them, and re-layouts  13.9 us
  transfers between devices with their start and end apart: 10, of which 10 were waited for; matrix products, arithmetic and copies ran while one was open for 7% of the time, Pallas kernels for 0%

profile of v1, /device:TPU:24, one launch (start us, length us, event | category | flops | bytes accessed | tf_op | source)
XLA Modules:
  0.0 600.9 jit_solution(15200731028337561219)
XLA Ops:
  0.6 0.9 copy.406
  1.6 0.9 copy.407
  2.5 0.9 copy.408
  3.5 0.9 copy.409
  4.5 0.9 copy.284
  5.5 4.3 all-to-all-start
  10.5 9.6 %all-to-all-done = bf16[16,4,8,512]{3,0,1,2:T(8,128)(2,1)S(1)} async-done(((bf16[16,4,8,512]{3,0,1,2:T(8,128)(2,1)}), bf16[16,4,8,512]{3,0,1,2:T(8,128)(2,1)S(1)}, u32[]{:S(2)}, u32[]{:S(2)}) %all-to-all-start) | async-done | bytes 524320 | tf_op jit(solution)/shard_map/all_to_all | solution.py:48
  21.7 2.2 reduce.18
  23.9 0.9 reshape.494
  24.8 18.5 %all-to-all-start.2 = ((bf16[64,2,1024]{2,1,0:T(2,128)(2,1)}), bf16[64,2,1024]{2,1,0:T(2,128)(2,1)S(1)}, u32[]{:S(2)}, u32[]{:S(2)}) async-start(bf16[64,2,1024]{2,1,0:T(2,128)(2,1)} %reshape.494), calls=%async_computation.2 | async-start | bytes 524288 | tf_op jit(solution)/shard_map/all_to_all | solution.py:29
  43.7 0.7 fusion.81
  44.4 20.1 %all-to-all-done.2 = bf16[64,2,1024]{2,1,0:T(2,128)(2,1)S(1)} async-done(((bf16[64,2,1024]{2,1,0:T(2,128)(2,1)}), bf16[64,2,1024]{2,1,0:T(2,128)(2,1)S(1)}, u32[]{:S(2)}, u32[]{:S(2)}) %all-to-all-start.2) | async-done | bytes 262176 | tf_op jit(solution)/shard_map/all_to_all | solution.py:29
  65.5 2.2 reduce.19
  67.7 0.9 reshape.496
  68.6 5.9 all-to-all-start.3
  74.9 2.8 gather_fusion
  77.7 4.6 broadcast_select_fusion
  82.3 12.9 %all-to-all-done.3 = bf16[64,2,1024]{2,1,0:T(2,128)(2,1)S(1)} async-done(((bf16[64,2,1024]{2,1,0:T(2,128)(2,1)}), bf16[64,2,1024]{2,1,0:T(2,128)(2,1)S(1)}, u32[]{:S(2)}, u32[]{:S(2)}) %all-to-all-start.3) | async-done | bytes 262176 | tf_op jit(solution)/shard_map/all_to_all | solution.py:36
  95.2 6.7 %all-to-all-start.1 = ((bf16[64,32,1024]{2,1,0:T(8,128)(2,1)}), bf16[64,32,1024]{2,1,0:T(8,128)(2,1)}, u32[]{:S(2)}, u32[]{:S(2)}) async-start(bf16[64,32,1024]{2,1,0:T(8,128)(2,1)} %broadcast_select_fusion), calls=%async_computation.1 | async-start | bytes 8388608 | tf_op jit(solution)/shard_map/all_to_all | solution.py:89
  102.5 3.4 collective-permute-start
  105.9 2.5 collective-permute-start.1
  108.4 170.6 %collective-permute-done = bf16[32,1024]{1,0:T(8,128)(2,1)S(1)} collective-permute-done((bf16[32,1024]{1,0:T(8,128)(2,1)S(1)}, bf16[32,1024]{1,0:T(8,128)(2,1)S(1)}, u32[]{:S(2)}, u32[]{:S(2)}) %collective-permute-start) | collective-permute-done | bytes 65568 | tf_op jit(solution)/shard_map/ppermute | solution.py:21
  279.1 2.5 collective-permute-done.1
  281.6 0.7 reshape.497
  282.3 1.5 reduce.15
  284.0 0.7 slice_bitcast_fusion.8
  286.8 1.2 reshape.412
  288.0 3.2 all-to-all-done.1
  291.2 2.8 gather_fusion.1
  294.3 1.2 slice_bitcast_fusion.1
  295.5 1.3 fusion.15
  296.8 1.2 copy.304
  300.6 0.7 copy.480
  301.4 1.5 reshape.413
  302.8 1.3 fusion.13
  304.1 1.2 copy.311
  305.3 1.3 reshape.410
  306.6 2.1 fusion.11
  311.2 44.3 %all_to_all.56 = f32[64,1,2048]{2,1,0:T(1,128)S(1)} all-to-all(f32[64,1,2048]{2,1,0:T(1,128)S(1)} %all_to_all.48), channel_id=1, replica_groups=mesh['ctx'=64,'head'=8] {'ctx'}, dimensions={0} | all-to-all | bytes 1048576 | tf_op jit(solution)/shard_map/all_to_all | solution.py:29
  355.8 1.1 broadcast_in_dim.111
  356.9 5.9 all-to-all-start.5
  362.8 1.3 fusion.83
  365.0 0.9 concatenate.87
  366.4 1.3 fusion.84
  368.6 0.9 concatenate.86
  369.5 1.1 pad_maximum_fusion.1
  370.6 2.5 broadcast_in_dim.112
  373.1 2.8 scatter_fusion
  375.9 18.8 %all-to-all-done.5 = f32[64,1,2048]{2,1,0:T(1,128)S(1)} async-done(((f32[64,1,2048]{2,1,0:T(1,128)}), f32[64,1,2048]{2,1,0:T(1,128)S(1)}, u32[]{:S(2)}, u32[]{:S(2)}) %all-to-all-start.5) | async-done | bytes 524320 | tf_op jit(solution)/shard_map/all_to_all | solution.py:36
  394.7 0.8 copy-done.4
  395.5 6.1 %all-to-all-start.6 = ((bf16[64,32,1024]{2,1,0:T(8,128)(2,1)}), bf16[64,32,1024]{2,1,0:T(8,128)(2,1)}, u32[]{:S(2)}, u32[]{:S(2)}) async-start(bf16[64,32,1024]{2,1,0:T(8,128)(2,1)} %scatter_fusion), calls=%async_computation.6 | async-start | bytes 8388608 | tf_op jit(solution)/shard_map/all_to_all | solution.py:187
  403.3 1.3 copy.387
  405.4 1.2 reshape.486
  406.6 1.2 constant_dynamic-update-slice_fusion.1
  408.1 3.5 collective-permute-start.2
  411.6 2.7 collective-permute-start.3
  416.0 163.6 %collective-permute-done.2 = bf16[32,1024]{1,0:T(8,128)(2,1)S(1)} collective-permute-done((bf16[32,1024]{1,0:T(8,128)(2,1)S(1)}, bf16[32,1024]{1,0:T(8,128)(2,1)S(1)}, u32[]{:S(2)}, u32[]{:S(2)}) %collective-permute-start.2) | collective-permute-done | bytes 65568 | tf_op jit(solution)/shard_map/ppermute | solution.py:21
  579.6 2.4 collective-permute-done.3
  582.6 1.1 scatter-add.9
  583.7 1.2 reduce.16
  585.0 6.6 %all-to-all-done.6 = bf16[64,32,1024]{2,1,0:T(8,128)(2,1)} async-done(((bf16[64,32,1024]{2,1,0:T(8,128)(2,1)}), bf16[64,32,1024]{2,1,0:T(8,128)(2,1)}, u32[]{:S(2)}, u32[]{:S(2)}) %all-to-all-start.6) | async-done | bytes 4194336 | tf_op jit(solution)/shard_map/all_to_all | solution.py:187
  591.6 6.7 %fusion = f32[4,32,1024]{2,0,1:T(4,128)S(1)} fusion(bf16[64,32,1024]{2,1,0:T(8,128)(2,1)} %all-to-all-done.6, s32[64]{0:T(128)S(1)} %copy-done.15, pred[64]{0:T(512)(128)(4,1)S(1)} %reduce_or.18), kind=kOutput, calls=%fused_computation.4 | convolution fusion | flops 16777728 | bytes 4718912 | tf_op jit(solution)/shard_map/jr,rkc->jkc/dot_general | solution.py:219
  598.3 1.0 fusion.3
  599.3 0.7 copy.352
  (155 shorter events, 20.3 us)
Async XLA Ops:
  4.4 5.4 copy-start.21
  4.4 5.4 copy-start.13
  5.5 14.6 %all-to-all-start = ((bf16[16,4,8,512]{3,0,1,2:T(8,128)(2,1)}), bf16[16,4,8,512]{3,0,1,2:T(8,128)(2,1)S(1)}, u32[]{:S(2)}, u32[]{:S(2)}) async-start(bf16[16,4,8,512]{3,0,1,2:T(8,128)(2,1)} %copy.284), calls=%async_computation | async-start | bytes 1048576 | tf_op jit(solution)/shard_map/all_to_all | solution.py:48
  9.8 10.4 %copy-start.16 = (s32[4]{0:T(128)}, s32[4]{0:T(128)S(1)}, u32[]{:S(2)}) copy-start(s32[4]{0:T(128)S(1)} %get-tuple-element.30) | copy-start | bytes 52
  10.5 10.3 %copy-start.18 = (s32[12]{0:T(128)}, s32[12]{0:T(128)S(1)}, u32[]{:S(2)}) copy-start(s32[12]{0:T(128)S(1)} %fusion.79) | copy-start | bytes 148
  24.8 39.8 %all-to-all-start.2 = ((bf16[64,2,1024]{2,1,0:T(2,128)(2,1)}), bf16[64,2,1024]{2,1,0:T(2,128)(2,1)S(1)}, u32[]{:S(2)}, u32[]{:S(2)}) async-start(bf16[64,2,1024]{2,1,0:T(2,128)(2,1)} %reshape.494), calls=%async_computation.2 | async-start | bytes 524288 | tf_op jit(solution)/shard_map/all_to_all | solution.py:29
  68.6 26.6 %all-to-all-start.3 = ((bf16[64,2,1024]{2,1,0:T(2,128)(2,1)}), bf16[64,2,1024]{2,1,0:T(2,128)(2,1)S(1)}, u32[]{:S(2)}, u32[]{:S(2)}) async-start(bf16[64,2,1024]{2,1,0:T(2,128)(2,1)} %reshape.496), calls=%async_computation.3 | async-start | bytes 524288 | tf_op jit(solution)/shard_map/all_to_all | solution.py:36
  74.9 2.9 copy-start.14
  95.2 195.9 %all-to-all-start.1 = ((bf16[64,32,1024]{2,1,0:T(8,128)(2,1)}), bf16[64,32,1024]{2,1,0:T(8,128)(2,1)}, u32[]{:S(2)}, u32[]{:S(2)}) async-start(bf16[64,32,1024]{2,1,0:T(8,128)(2,1)} %broadcast_select_fusion), calls=%async_computation.1 | async-start | bytes 8388608 | tf_op jit(solution)/shard_map/all_to_all | solution.py:89
  102.5 176.5 %collective-permute-start = (bf16[32,1024]{1,0:T(8,128)(2,1)S(1)}, bf16[32,1024]{1,0:T(8,128)(2,1)S(1)}, u32[]{:S(2)}, u32[]{:S(2)}) collective-permute-start(bf16[32,1024]{1,0:T(8,128)(2,1)S(1)} %get-tuple-element.55), channel_id=1, source_target_pairs={{0,8},{8,16},{16,24},{24,32},{32,40},{40,48},{48,56},{56,64},{64,7... | collective-permute-start | bytes 196616 | tf_op jit(solution)/shard_map/ppermute | solution.py:21
  105.9 175.6 %collective-permute-start.1 = (bf16[32,1024]{1,0:T(8,128)(2,1)S(1)}, bf16[32,1024]{1,0:T(8,128)(2,1)S(1)}, u32[]{:S(2)}, u32[]{:S(2)}) collective-permute-start(bf16[32,1024]{1,0:T(8,128)(2,1)S(1)} %get-tuple-element.56), channel_id=1, source_target_pairs={{8,0},{16,8},{24,16},{32,24},{40,32},{48,40},{56,48},{64,56},{72,6... | collective-permute-start | bytes 196616 | tf_op jit(solution)/shard_map/ppermute | solution.py:22
  295.5 1.3 copy-start.1
  300.4 2.5 copy-start.3
  306.6 2.1 copy-start.7
  306.6 2.1 copy-start.10
  309.4 53.4 %copy-start.9 = (bf16[4,4,32,320]{3,2,1,0:T(8,128)(2,1)}, bf16[4,4,32,320]{3,2,1,0:T(8,128)(2,1)S(1)}, u32[]{:S(2)}) copy-start(bf16[4,4,32,320]{3,2,1,0:T(8,128)(2,1)S(1)} %fusion.20) | copy-start | bytes 983044
  309.4 1.1 copy-start.11
  355.5 7.4 %copy-start = (bf16[4,4,32,6,32]{4,3,2,1,0:T(8,128)(2,1)S(1)}, bf16[4,4,32,6,32]{4,3,2,1,0:T(8,128)(2,1)}, u32[]{:S(2)}) copy-start(bf16[4,4,32,6,32]{4,3,2,1,0:T(8,128)(2,1)} %reshape.413) | copy-start | bytes 589828
  356.9 37.8 %all-to-all-start.5 = ((f32[64,1,2048]{2,1,0:T(1,128)}), f32[64,1,2048]{2,1,0:T(1,128)S(1)}, u32[]{:S(2)}, u32[]{:S(2)}) async-start(f32[64,1,2048]{2,1,0:T(1,128)} %broadcast_in_dim.111), calls=%async_computation.5 | async-start | bytes 1048576 | tf_op jit(solution)/shard_map/all_to_all | solution.py:36
  364.7 1.2 slice-start
  368.3 1.2 copy-start.8
  370.6 2.5 copy-start.19
  375.9 25.7 %copy-start.20 = (pred[256]{0:T(512)(128)(4,1)S(1)}, pred[256]{0:T(512)(128)(4,1)}, u32[]{:S(2)}) copy-start(pred[256]{0:T(512)(128)(4,1)} %get-tuple-element.27) | copy-start | bytes 772
  375.9 26.0 %copy-start.6 = (bf16[4,4,32,3,32]{4,3,2,1,0:T(4,128)(2,1)S(1)}, bf16[4,4,32,3,32]{4,3,2,1,0:T(4,128)(2,1)}, u32[]{:S(2)}) copy-start(bf16[4,4,32,3,32]{4,3,2,1,0:T(4,128)(2,1)} %get-tuple-element.35) | copy-start | bytes 294916
  394.7 0.8 copy-start.4
  395.5 196.0 %all-to-all-start.6 = ((bf16[64,32,1024]{2,1,0:T(8,128)(2,1)}), bf16[64,32,1024]{2,1,0:T(8,128)(2,1)}, u32[]{:S(2)}, u32[]{:S(2)}) async-start(bf16[64,32,1024]{2,1,0:T(8,128)(2,1)} %scatter_fusion), calls=%async_computation.6 | async-start | bytes 8388608 | tf_op jit(solution)/shard_map/all_to_all | solution.py:187
  407.9 6.4 %copy-start.12 = (bf16[4,4,4,8,128]{4,3,2,1,0:T(8,128)(2,1)S(1)}, bf16[4,4,4,8,128]{4,3,2,1,0:T(8,128)(2,1)}, u32[]{:S(2)}) copy-start(bf16[4,4,4,8,128]{4,3,2,1,0:T(8,128)(2,1)} %get-tuple-element.49) | copy-start | bytes 393220
  408.0 6.6 %copy-start.2 = (bf16[4,6,4,4,8,128]{5,4,3,2,1,0:T(8,128)(2,1)S(1)}, bf16[4,6,4,4,8,128]{5,4,3,2,1,0:T(8,128)(2,1)}, u32[]{:S(2)}) copy-start(bf16[4,6,4,4,8,128]{5,4,3,2,1,0:T(8,128)(2,1)} %copy-done.1) | copy-start | bytes 2359300
  408.1 171.5 %collective-permute-start.2 = (bf16[32,1024]{1,0:T(8,128)(2,1)S(1)}, bf16[32,1024]{1,0:T(8,128)(2,1)S(1)}, u32[]{:S(2)}, u32[]{:S(2)}) collective-permute-start(bf16[32,1024]{1,0:T(8,128)(2,1)S(1)} %get-tuple-element.39), channel_id=1, source_target_pairs={{0,8},{8,16},{16,24},{24,32},{32,40},{40,48},{48,56},{56,64},{64,7... | collective-permute-start | bytes 196616 | tf_op jit(solution)/shard_map/ppermute | solution.py:21
  411.6 170.4 %collective-permute-start.3 = (bf16[32,1024]{1,0:T(8,128)(2,1)S(1)}, bf16[32,1024]{1,0:T(8,128)(2,1)S(1)}, u32[]{:S(2)}, u32[]{:S(2)}) collective-permute-start(bf16[32,1024]{1,0:T(8,128)(2,1)S(1)} %get-tuple-element.40), channel_id=1, source_target_pairs={{8,0},{16,8},{24,16},{32,24},{40,32},{48,40},{56,48},{64,56},{72,6... | collective-permute-start | bytes 196616 | tf_op jit(solution)/shard_map/ppermute | solution.py:22
  415.3 168.4 %copy-start.5 = (f32[64,1,2048]{2,1,0:T(1,128)S(1)}, f32[64,1,2048]{2,1,0:T(1,128)}, u32[]{:S(2)}) copy-start(f32[64,1,2048]{2,1,0:T(1,128)} %copy-done.4) | copy-start | bytes 1572868
  582.4 9.2 %copy-start.15 = (s32[64]{0:T(128)S(1)}, s32[64]{0:T(128)}, u32[]{:S(2)}) copy-start(s32[64]{0:T(128)} %copy-done.14) | copy-start | bytes 772
  585.0 13.3 %copy-start.17 = (s32[4]{0:T(128)S(1)}, s32[4]{0:T(128)}, u32[]{:S(2)}) copy-start(s32[4]{0:T(128)} %copy-done.16) | copy-start | bytes 52

commit v2 on v1

--- a/solution.py
+++ b/solution.py
@@ -1,6 +1,7 @@
 import math
 
 import jax
+import numpy as np
 import jax.numpy as jnp
 from jax import lax
 from jax.sharding import PartitionSpec as P
@@ -11,17 +12,14 @@
 NG = 4
 
 
-def with_halo(x, sides, width):
-    for axis, dim in sides:
-        peers, length = (lax.axis_size(axis), x.shape[dim])
-        up = [(i, (i + 1) % peers) for i in range(peers - 1)]
-        down = [(j, i) for i, j in up]
-        last = lax.slice_in_dim(x, length - width, length, axis=dim)
-        first = lax.slice_in_dim(x, 0, width, axis=dim)
-        before = lax.ppermute(last, axis, up)
-        after = lax.ppermute(first, axis, down)
-        x = jnp.concatenate([before, x, after], axis=dim)
-    return x
+def with_halo(x, axis, order, width):
+    ranges = len(order)
+    up = [(order[i], order[i + 1]) for i in range(ranges - 1)]
+    down = [(j, i) for i, j in up]
+    length = x.shape[0]
+    before = lax.ppermute(x[length - width :], axis, up)
+    after = lax.ppermute(x[:width], axis, down)
+    return jnp.concatenate([before, x, after], axis=0)
 
 
 def chunk_sum(x, axis):
@@ -40,26 +38,41 @@
     return chunk_share(chunk_sum(x, axis), axis, x.shape, x.dtype)
 
 
+SEQ_AXES = ("zl", "y", "x")
+SWAP_AXES = ("zh", "x")
+
+
+def swap_places(x):
+    side = lax.axis_size("x")
+    pairs = [(a * side + b, b * side + a) for a in range(side) for b in range(side)]
+    return lax.ppermute(x, SWAP_AXES, pairs)
+
+
 def per_device(queries, key_states, value_states, out_grad, random_blocks, global_blocks):
-    groups = lax.axis_size("head")
+    groups = lax.axis_size(("x", "core"))
     rows_in, cols_in = queries.shape
     stacked = jnp.stack([queries, key_states, value_states, out_grad], axis=1)
     stacked = stacked.reshape(rows_in, 4, groups, cols_in // groups)
-    stacked = lax.all_to_all(stacked, "head", split_axis=2, concat_axis=0, tiled=True)
+    stacked = lax.all_to_all(stacked, ("x", "core"), split_axis=2, concat_axis=0, tiled=True)
+    stacked = swap_places(stacked)
     query_rows, key_rows, value_rows, grad_rows = (stacked[:, i, 0] for i in range(4))
     tokens = query_rows.shape[0]
     head_cols = query_rows.shape[1]
     heads_here = head_cols // DH
     blocks_here = tokens // BS
-    devices = lax.axis_size("ctx")
-    my_index = lax.axis_index("ctx")
+    lz, ly, lx = (lax.axis_size(a) for a in SEQ_AXES)
+    devices = lz * ly * lx
+    my_index = (lax.axis_index("x") * lz + lax.axis_index("zl")) * ly + lax.axis_index("y")
+    order = [((r // ly) % lz) * (ly * lx) + (r % ly) * lx + r // (lz * ly) for r in range(devices)]
+    range_at = np.argsort(np.array(order)).astype(np.int32)
+    slot_of = jnp.array(order, jnp.int32)
     total_blocks = devices * blocks_here
     entries = blocks_here * NR
     capacity = (entries + devices - 1) // devices
     inv_root = 1.0 / math.sqrt(DH)
     kv_rows = jnp.concatenate([key_rows, value_rows], axis=1)
     kv_blocks = kv_rows.reshape(blocks_here, BS, 2 * head_cols)
-    extended = with_halo(kv_rows, (("ctx", 0),), BS)
+    extended = with_halo(kv_rows, SEQ_AXES, order, BS)
     extended = extended.reshape(blocks_here + 2, BS, 2 * head_cols)
     window = jnp.stack(
         [extended[:blocks_here], extended[1 : blocks_here + 1], extended[2:]], axis=1
@@ -68,7 +81,7 @@
     global_offset = global_blocks % blocks_here
     owned = jnp.take(kv_blocks, global_offset, axis=0)
     owned = jnp.where((global_owner == my_index)[:, None, None], owned, jnp.zeros_like(owned))
-    global_kv = all_sum(owned, "ctx")
+    global_kv = all_sum(owned, SEQ_AXES)
     entry_table = random_blocks.reshape(devices, entries)
     table_owner = entry_table // blocks_here
     table_offset = entry_table % blocks_here
@@ -78,15 +91,15 @@
     table_slot = jnp.sum(matches.astype(jnp.int32), axis=2)
     my_owner = lax.dynamic_index_in_dim(table_owner, my_index, 0, keepdims=False)
     my_slot = lax.dynamic_index_in_dim(table_slot, my_index, 0, keepdims=False)
-    my_target = my_owner * capacity + my_slot
+    my_target = slot_of[my_owner] * capacity + my_slot
     slot_ids = jnp.arange(capacity, dtype=jnp.int32)
     served = (table_owner == my_index)[:, :, None] & (
         table_slot[:, :, None] == slot_ids[None, None, :]
     )
-    served_block = jnp.sum(jnp.where(served, table_offset[:, :, None], 0), axis=1).reshape(-1)
-    served_used = jnp.any(served, axis=1).reshape(-1)
+    served_block = jnp.sum(jnp.where(served, table_offset[:, :, None], 0), axis=1)[range_at].reshape(-1)
+    served_used = jnp.any(served, axis=1)[range_at].reshape(-1)
     outgoing = jnp.take(kv_blocks, served_block, axis=0)
-    incoming = lax.all_to_all(outgoing, "ctx", split_axis=0, concat_axis=0, tiled=True)
+    incoming = lax.all_to_all(outgoing, SEQ_AXES, split_axis=0, concat_axis=0, tiled=True)
     fetched = jnp.take(incoming, my_target, axis=0).reshape(blocks_here, NR, BS, 2 * head_cols)
     near_kv = jnp.concatenate([window, fetched], axis=1)
     near_groups = 3 + NR
@@ -184,7 +197,7 @@
         .at[my_target]
         .set(random_part)
     )
-    arrived = lax.all_to_all(back_rows, "ctx", split_axis=0, concat_axis=0, tiled=True)
+    arrived = lax.all_to_all(back_rows, SEQ_AXES, split_axis=0, concat_axis=0, tiled=True)
     window_part = key_value_parts(near_ds[:, :, :, :3], near_probs[:, :, :, :3])
     zero_block = jnp.zeros((1, BS, 2 * head_cols), jnp.float32)
     own_grad = (
@@ -193,7 +206,7 @@
         + jnp.concatenate([zero_block, window_part[:-1, 2]], axis=0)
     )
     rims_out = jnp.concatenate([window_part[0, 0], window_part[blocks_here - 1, 2]], axis=0)
-    rims_in = with_halo(rims_out.astype(jnp.bfloat16), (("ctx", 0),), BS).astype(rims_out.dtype)
+    rims_in = with_halo(rims_out.astype(jnp.bfloat16), SEQ_AXES, order, BS).astype(rims_out.dtype)
     own_grad = own_grad.at[0].add(rims_in[:BS]).at[blocks_here - 1].add(rims_in[3 * BS :])
     far_key = (
         jnp.einsum("bhqgk,bqhd->gkhd", far_ds, query_heads, preferred_element_type=jnp.float32)
@@ -205,7 +218,7 @@
     far_part = jnp.concatenate(
         [far_key.reshape(NG, BS, head_cols), far_value.reshape(NG, BS, head_cols)], axis=2
     )
-    far_sum = all_sum(far_part, "ctx")
+    far_sum = all_sum(far_part, SEQ_AXES)
     here_ids = jnp.arange(blocks_here, dtype=jnp.int32)
     own_global = (
         (global_owner == my_index)[None, :] & (global_offset[None, :] == here_ids[:, None])
@@ -221,22 +234,20 @@
     )
     key_grad = own_grad[..., :head_cols].astype(jnp.bfloat16).reshape(tokens, head_cols)
     value_grad = own_grad[..., head_cols:].astype(jnp.bfloat16).reshape(tokens, head_cols)
-    return (query_grad, key_grad, value_grad)
+    return tuple(swap_places(out) for out in (query_grad, key_grad, value_grad))
 
 
 def solution(mesh):
-    placed = (
-        P(("ctx", "head"), None),
-        P(("ctx", "head"), None),
-        P(("ctx", "head"), None),
-        P(("ctx", "head"), None),
-        P(),
-        P(),
-    )
+    side = mesh.devices.shape[1] // 2
+    grid = mesh.devices.reshape(-1, mesh.devices.shape[0] // (side * side), side, side, 2)
+    cube = jax.sharding.Mesh(grid, ("zh", "zl", "y", "x", "core"))
+    rows = ("zh", "zl", "y", "x", "core")
+    placed = (P(rows, None),) * 4 + (P(), P())
+    out = P(("zh", "zl", "y"), ("x", "core"))
     return jax.shard_map(
         per_device,
-        mesh=mesh,
+        mesh=cube,
         in_specs=placed,
-        out_specs=(P("ctx", "head"), P("ctx", "head"), P("ctx", "head")),
+        out_specs=(out, out, out),
         check_vma=False,
     )

time: 610 us -> 491 us (0.80)
  the two profiles are of different devices: /device:TPU:24 before, /device:TPU:2 now
where the time goes in v2:
time: 491 us; the launch traced here: 482 us
  waiting for transfers between devices  274 us (56%)
  starting transfers between devices  91.1 us (19%)
  local copies, waits for them, and re-layouts  53.3 us (11%)
  blocking collectives  27.8 us (6%)
  other arithmetic  18 us (4%)
  matrix products  15.6 us (3%)
    ppermute x2, waiting for transfers between devices, with_halo(): before = lax.ppermute(x[length - width:], axis, up)  122 us
    ppermute x4, waiting for transfers between devices, swap_places(): return lax.ppermute(x, SWAP_AXES, pairs)  100 us
    all_to_all x1, blocking collectives, chunk_sum(): lax.all_to_all(x.reshape(peers, -1), axis, split_axis=0, concat_axis=0, t...  27.8 us
    ppermute x4, starting transfers between devices, swap_places(): return lax.ppermute(x, SWAP_AXES, pairs)  21 us
    all_to_all x1, waiting for transfers between devices, per_device(): lax.all_to_all(outgoing, SEQ_AXES, split_axis=0, concat_axis=0, tiled=True)  14.8 us
    ppermute x2, starting transfers between devices, with_halo(): after = lax.ppermute(x[:width], axis, down)  14.5 us
    all_to_all x1, waiting for transfers between devices, per_device(): lax.all_to_all(back_rows, SEQ_AXES, split_axis=0, concat_axis=0, tiled=True)  14.4 us
    unnamed x74, local copies, waits for them, and re-layouts  13.5 us
  transfers between devices with their start and end apart: 14, of which 11 were waited for; matrix products, arithmetic and copies ran while one was open for 10% of the time, Pallas kernels for 0%

profile of v2, /device:TPU:2, one launch (start us, length us, event | category | flops | bytes accessed | tf_op | source)
XLA Modules:
  0.0 481.9 jit_solution(4540129481221821142)
XLA Ops:
  0.6 0.9 copy.410
  1.6 0.9 copy.411
  2.5 0.9 copy.412
  3.5 0.9 copy.413
  4.5 1.0 copy.288
  5.5 9.3 %all-to-all-start = ((bf16[16,4,8,512]{3,0,1,2:T(8,128)(2,1)}), bf16[16,4,8,512]{3,0,1,2:T(8,128)(2,1)S(1)}, u32[]{:S(2)}, u32[]{:S(2)}) async-start(bf16[16,4,8,512]{3,0,1,2:T(8,128)(2,1)} %copy.288), calls=%async_computation | async-start | bytes 1048576 | tf_op jit(solution)/shard_map/all_to_all | solution.py:56
  16.4 7.3 %all-to-all-done = bf16[16,4,8,512]{3,0,1,2:T(8,128)(2,1)S(1)} async-done(((bf16[16,4,8,512]{3,0,1,2:T(8,128)(2,1)}), bf16[16,4,8,512]{3,0,1,2:T(8,128)(2,1)S(1)}, u32[]{:S(2)}, u32[]{:S(2)}) %all-to-all-start) | async-done | bytes 524320 | tf_op jit(solution)/shard_map/all_to_all | solution.py:56
  23.8 5.5 %collective-permute-start = (bf16[128,4,1,512]{3,0,1,2:T(8,128)(2,1)S(1)}, bf16[128,4,1,512]{3,0,1,2:T(8,128)(2,1)S(1)}, u32[]{:S(2)}, u32[]{:S(2)}) collective-permute-start(bf16[128,4,1,512]{3,0,1,2:T(8,128)(2,1)S(1)} %bitcast.256), channel_id=1, source_target_pairs={{0,0},{2,128},{4,256},{6,384},{128,2},{130,130},{132,258},{134,386... | collective-permute-start | bytes 1572872 | tf_op jit(solution)/shard_map/ppermute | solution.py:48
  29.3 69.2 %collective-permute-done = bf16[128,4,1,512]{3,0,1,2:T(8,128)(2,1)S(1)} collective-permute-done((bf16[128,4,1,512]{3,0,1,2:T(8,128)(2,1)S(1)}, bf16[128,4,1,512]{3,0,1,2:T(8,128)(2,1)S(1)}, u32[]{:S(2)}, u32[]{:S(2)}) %collective-permute-start) | collective-permute-done | bytes 524320 | tf_op jit(solution)/shard_map/ppermute | solution.py:48
  100.1 2.2 reduce.20
  102.2 0.9 reshape.552
  103.1 11.3 %all-to-all-start.2 = ((bf16[64,2,1024]{2,1,0:T(2,128)(2,1)}), bf16[64,2,1024]{2,1,0:T(2,128)(2,1)S(1)}, u32[]{:S(2)}, u32[]{:S(2)}) async-start(bf16[64,2,1024]{2,1,0:T(2,128)(2,1)} %reshape.552), calls=%async_computation.2 | async-start | bytes 524288 | tf_op jit(solution)/shard_map/all_to_all | solution.py:27
  115.8 10.0 %all-to-all-done.2 = bf16[64,2,1024]{2,1,0:T(2,128)(2,1)S(1)} async-done(((bf16[64,2,1024]{2,1,0:T(2,128)(2,1)}), bf16[64,2,1024]{2,1,0:T(2,128)(2,1)S(1)}, u32[]{:S(2)}, u32[]{:S(2)}) %all-to-all-start.2) | async-done | bytes 262176 | tf_op jit(solution)/shard_map/all_to_all | solution.py:27
  126.8 2.2 reduce.21
  128.9 0.9 reshape.554
  129.8 6.0 %all-to-all-start.3 = ((bf16[64,2,1024]{2,1,0:T(2,128)(2,1)}), bf16[64,2,1024]{2,1,0:T(2,128)(2,1)S(1)}, u32[]{:S(2)}, u32[]{:S(2)}) async-start(bf16[64,2,1024]{2,1,0:T(2,128)(2,1)} %reshape.554), calls=%async_computation.3 | async-start | bytes 524288 | tf_op jit(solution)/shard_map/all_to_all | solution.py:34
  136.9 2.8 gather_fusion.2
  139.7 4.6 broadcast_select_fusion
  144.3 2.6 all-to-all-done.3
  146.9 8.3 %all-to-all-start.1 = ((bf16[64,32,1024]{2,1,0:T(8,128)(2,1)}), bf16[64,32,1024]{2,1,0:T(8,128)(2,1)}, u32[]{:S(2)}, u32[]{:S(2)}) async-start(bf16[64,32,1024]{2,1,0:T(8,128)(2,1)} %broadcast_select_fusion), calls=%async_computation.1 | async-start | bytes 8388608 | tf_op jit(solution)/shard_map/all_to_all | solution.py:102
  155.9 3.4 collective-permute-start.1
  159.3 7.3 %collective-permute-start.2 = (bf16[32,1024]{1,0:T(8,128)(2,1)S(1)}, bf16[32,1024]{1,0:T(8,128)(2,1)S(1)}, u32[]{:S(2)}, u32[]{:S(2)}) collective-permute-start(bf16[32,1024]{1,0:T(8,128)(2,1)S(1)} %get-tuple-element.56), channel_id=1, source_target_pairs={{8,0},{16,8},{24,16},{32,24},{40,32},{48,40},{56,48},{64,56},{72,6... | collective-permute-start | bytes 196616 | tf_op jit(solution)/shard_map/ppermute | solution.py:21
  166.6 62.5 %collective-permute-done.1 = bf16[32,1024]{1,0:T(8,128)(2,1)S(1)} collective-permute-done((bf16[32,1024]{1,0:T(8,128)(2,1)S(1)}, bf16[32,1024]{1,0:T(8,128)(2,1)S(1)}, u32[]{:S(2)}, u32[]{:S(2)}) %collective-permute-start.1) | collective-permute-done | bytes 65568 | tf_op jit(solution)/shard_map/ppermute | solution.py:20
  229.9 1.5 reduce.16
  234.3 1.2 reshape.437
  235.5 14.8 %all-to-all-done.1 = bf16[64,32,1024]{2,1,0:T(8,128)(2,1)} async-done(((bf16[64,32,1024]{2,1,0:T(8,128)(2,1)}), bf16[64,32,1024]{2,1,0:T(8,128)(2,1)}, u32[]{:S(2)}, u32[]{:S(2)}) %all-to-all-start.1) | async-done | bytes 4194336 | tf_op jit(solution)/shard_map/all_to_all | solution.py:102
  250.3 2.8 gather_fusion.3
  253.4 1.2 slice_bitcast_fusion.1
  254.7 1.3 fusion.13
  256.0 1.2 copy.308
  260.5 1.5 reshape.438
  262.0 1.3 fusion.11
  263.3 1.2 copy.315
  264.5 1.3 reshape.435
  265.7 2.1 multiply_reduce_fusion
  270.3 27.8 %all_to_all.56 = f32[64,1,2048]{2,1,0:T(1,128)S(1)} all-to-all(f32[64,1,2048]{2,1,0:T(1,128)S(1)} %all_to_all.48), channel_id=1, replica_groups=mesh['zh'=4,'zl'=4,'y'=4,'x'=4,'core'=2] {'zl','y','x'}, dimensions={0} | all-to-all | bytes 1048576 | tf_op jit(solution)/shard_map/all_to_all | solution.py:27
  298.4 1.1 broadcast_in_dim.119
  299.5 6.0 %all-to-all-start.5 = ((f32[64,1,2048]{2,1,0:T(1,128)}), f32[64,1,2048]{2,1,0:T(1,128)S(1)}, u32[]{:S(2)}, u32[]{:S(2)}) async-start(f32[64,1,2048]{2,1,0:T(1,128)} %broadcast_in_dim.119), calls=%async_computation.5 | async-start | bytes 1048576 | tf_op jit(solution)/shard_map/all_to_all | solution.py:34
  305.5 1.3 fusion.82
  307.7 0.9 concatenate.87
  309.0 1.4 fusion.83
  311.2 0.9 concatenate.86
  312.1 1.1 pad_maximum_fusion.1
  313.2 2.5 broadcast_in_dim.121
  315.8 2.8 scatter_fusion
  318.6 3.0 all-to-all-done.5
  321.6 0.8 copy-done.5
  322.4 7.9 %all-to-all-start.6 = ((bf16[64,32,1024]{2,1,0:T(8,128)(2,1)}), bf16[64,32,1024]{2,1,0:T(8,128)(2,1)}, u32[]{:S(2)}, u32[]{:S(2)}) async-start(bf16[64,32,1024]{2,1,0:T(8,128)(2,1)} %scatter_fusion), calls=%async_computation.6 | async-start | bytes 8388608 | tf_op jit(solution)/shard_map/all_to_all | solution.py:200
  330.6 0.8 gather_fusion.5
  331.9 1.4 copy.384
  333.3 1.5 reshape.544
  336.4 4.8 collective-permute-start.3
  342.7 3.4 collective-permute-start.4
  346.1 7.2 %collective-permute-start.5 = (bf16[32,1024]{1,0:T(8,128)(2,1)S(1)}, bf16[32,1024]{1,0:T(8,128)(2,1)S(1)}, u32[]{:S(2)}, u32[]{:S(2)}) collective-permute-start(bf16[32,1024]{1,0:T(8,128)(2,1)S(1)} %get-tuple-element.40), channel_id=1, source_target_pairs={{8,0},{16,8},{24,16},{32,24},{40,32},{48,40},{56,48},{64,56},{72,6... | collective-permute-start | bytes 196616 | tf_op jit(solution)/shard_map/ppermute | solution.py:21
  353.5 59.2 %collective-permute-done.4 = bf16[32,1024]{1,0:T(8,128)(2,1)S(1)} collective-permute-done((bf16[32,1024]{1,0:T(8,128)(2,1)S(1)}, bf16[32,1024]{1,0:T(8,128)(2,1)S(1)}, u32[]{:S(2)}, u32[]{:S(2)}) %collective-permute-start.4) | collective-permute-done | bytes 65568 | tf_op jit(solution)/shard_map/ppermute | solution.py:20
  413.4 1.1 scatter-add.9
  414.4 1.2 reduce.17
  415.8 14.4 %all-to-all-done.6 = bf16[64,32,1024]{2,1,0:T(8,128)(2,1)} async-done(((bf16[64,32,1024]{2,1,0:T(8,128)(2,1)}), bf16[64,32,1024]{2,1,0:T(8,128)(2,1)}, u32[]{:S(2)}, u32[]{:S(2)}) %all-to-all-start.6) | async-done | bytes 4194336 | tf_op jit(solution)/shard_map/all_to_all | solution.py:200
  430.2 6.7 %fusion = f32[4,32,1024]{2,0,1:T(4,128)S(1)} fusion(bf16[64,32,1024]{2,1,0:T(8,128)(2,1)} %all-to-all-done.6, s32[64]{0:T(128)S(1)} %copy-done.24, pred[64]{0:T(512)(128)(4,1)S(1)} %gather_fusion.5), kind=kOutput, calls=%fused_computation.7 | convolution fusion | flops 16777728 | bytes 4718912 | tf_op jit(solution)/shard_map/jr,rkc->jkc/dot_general | solution.py:232
  436.9 1.0 fusion.3
  438.0 8.2 %collective-permute-start.6 = (bf16[128,512]{1,0:T(8,128)(2,1)S(1)}, bf16[128,512]{1,0:T(8,128)(2,1)S(1)}, u32[]{:S(2)}, u32[]{:S(2)}) collective-permute-start(bf16[128,512]{1,0:T(8,128)(2,1)S(1)} %bitcast.268), channel_id=1, source_target_pairs={{0,0},{2,128},{4,256},{6,384},{128,2},{130,130},{132,258},{134,386... | collective-permute-start | bytes 393224 | tf_op jit(solution)/shard_map/ppermute | solution.py:48
  446.2 2.4 collective-permute-start.7
  448.7 29.6 %collective-permute-done.6 = bf16[128,512]{1,0:T(8,128)(2,1)S(1)} collective-permute-done((bf16[128,512]{1,0:T(8,128)(2,1)S(1)}, bf16[128,512]{1,0:T(8,128)(2,1)S(1)}, u32[]{:S(2)}, u32[]{:S(2)}) %collective-permute-start.6) | collective-permute-done | bytes 131104 | tf_op jit(solution)/shard_map/ppermute | solution.py:48
  478.3 1.4 collective-permute-done.7
  (184 shorter events, 25.8 us)
Async XLA Ops:
  4.4 10.4 %copy-start.15 = (s32[256,3]{0,1:T(4,128)S(1)}, s32[256,3]{0,1:T(4,128)}, u32[]{:S(2)}) copy-start(s32[256,3]{0,1:T(4,128)} %param.18) | copy-start | bytes 9220
  4.4 10.9 %copy-start = (s32[64]{0:T(128)S(1)}, s32[64]{0:T(128)}, u32[]{:S(2)}) copy-start(s32[64]{0:T(128)} %constant.188.clone) | copy-start | bytes 772
  4.5 11.8 %copy-start.25 = (s32[4]{0:T(128)S(1)}, s32[4]{0:T(128)}, u32[]{:S(2)}) copy-start(s32[4]{0:T(128)} %param.19) | copy-start | bytes 52
  5.5 18.2 %all-to-all-start = ((bf16[16,4,8,512]{3,0,1,2:T(8,128)(2,1)}), bf16[16,4,8,512]{3,0,1,2:T(8,128)(2,1)S(1)}, u32[]{:S(2)}, u32[]{:S(2)}) async-start(bf16[16,4,8,512]{3,0,1,2:T(8,128)(2,1)} %copy.288), calls=%async_computation | async-start | bytes 1048576 | tf_op jit(solution)/shard_map/all_to_all | solution.py:56
  16.4 82.2 %copy-start.18 = (s32[4]{0:T(128)}, s32[4]{0:T(128)S(1)}, u32[]{:S(2)}) copy-start(s32[4]{0:T(128)S(1)} %get-tuple-element.30) | copy-start | bytes 52
  16.4 82.8 %copy-start.16 = (pred[4]{0:T(512)(128)(4,1)}, pred[4]{0:T(512)(128)(4,1)S(1)}, u32[]{:S(2)}) copy-start(pred[4]{0:T(512)(128)(4,1)S(1)} %get-tuple-element.57) | copy-start | bytes 16
  23.8 74.7 %collective-permute-start = (bf16[128,4,1,512]{3,0,1,2:T(8,128)(2,1)S(1)}, bf16[128,4,1,512]{3,0,1,2:T(8,128)(2,1)S(1)}, u32[]{:S(2)}, u32[]{:S(2)}) collective-permute-start(bf16[128,4,1,512]{3,0,1,2:T(8,128)(2,1)S(1)} %bitcast.256), channel_id=1, source_target_pairs={{0,0},{2,128},{4,256},{6,384},{128,2},{130,130},{132,258},{134,386... | collective-permute-start | bytes 1572872 | tf_op jit(solution)/shard_map/ppermute | solution.py:48
  29.3 69.3 %copy-start.20 = (s32[12]{0:T(128)}, s32[12]{0:T(128)S(1)}, u32[]{:S(2)}) copy-start(s32[12]{0:T(128)S(1)} %fusion.78) | copy-start | bytes 148
  103.1 22.7 %all-to-all-start.2 = ((bf16[64,2,1024]{2,1,0:T(2,128)(2,1)}), bf16[64,2,1024]{2,1,0:T(2,128)(2,1)S(1)}, u32[]{:S(2)}, u32[]{:S(2)}) async-start(bf16[64,2,1024]{2,1,0:T(2,128)(2,1)} %reshape.552), calls=%async_computation.2 | async-start | bytes 524288 | tf_op jit(solution)/shard_map/all_to_all | solution.py:27
  126.0 9.8 %copy-start.26 = (s32[64]{0:T(128)S(1)}, s32[64]{0:T(128)}, u32[]{:S(2)}) copy-start(s32[64]{0:T(128)} %constant.200) | copy-start | bytes 772
  129.8 17.1 %all-to-all-start.3 = ((bf16[64,2,1024]{2,1,0:T(2,128)(2,1)}), bf16[64,2,1024]{2,1,0:T(2,128)(2,1)S(1)}, u32[]{:S(2)}, u32[]{:S(2)}) async-start(bf16[64,2,1024]{2,1,0:T(2,128)(2,1)} %reshape.554), calls=%async_computation.3 | async-start | bytes 524288 | tf_op jit(solution)/shard_map/all_to_all | solution.py:34
  136.9 2.8 copy-start.23
  146.9 103.4 %all-to-all-start.1 = ((bf16[64,32,1024]{2,1,0:T(8,128)(2,1)}), bf16[64,32,1024]{2,1,0:T(8,128)(2,1)}, u32[]{:S(2)}, u32[]{:S(2)}) async-start(bf16[64,32,1024]{2,1,0:T(8,128)(2,1)} %broadcast_select_fusion), calls=%async_computation.1 | async-start | bytes 8388608 | tf_op jit(solution)/shard_map/all_to_all | solution.py:102
  155.9 73.2 %collective-permute-start.1 = (bf16[32,1024]{1,0:T(8,128)(2,1)S(1)}, bf16[32,1024]{1,0:T(8,128)(2,1)S(1)}, u32[]{:S(2)}, u32[]{:S(2)}) collective-permute-start(bf16[32,1024]{1,0:T(8,128)(2,1)S(1)} %get-tuple-element.55), channel_id=1, source_target_pairs={{0,8},{8,16},{16,24},{24,32},{32,40},{40,48},{48,56},{56,64},{64,7... | collective-permute-start | bytes 196616 | tf_op jit(solution)/shard_map/ppermute | solution.py:20
  159.3 69.8 %collective-permute-start.2 = (bf16[32,1024]{1,0:T(8,128)(2,1)S(1)}, bf16[32,1024]{1,0:T(8,128)(2,1)S(1)}, u32[]{:S(2)}, u32[]{:S(2)}) collective-permute-start(bf16[32,1024]{1,0:T(8,128)(2,1)S(1)} %get-tuple-element.56), channel_id=1, source_target_pairs={{8,0},{16,8},{24,16},{32,24},{40,32},{48,40},{56,48},{64,56},{72,6... | collective-permute-start | bytes 196616 | tf_op jit(solution)/shard_map/ppermute | solution.py:21
  254.6 1.3 copy-start.2
  259.5 2.5 copy-start.4
  265.7 2.1 copy-start.9
  265.7 2.1 copy-start.12
  268.5 37.0 %copy-start.11 = (bf16[4,4,32,320]{3,2,1,0:T(8,128)(2,1)}, bf16[4,4,32,320]{3,2,1,0:T(8,128)(2,1)S(1)}, u32[]{:S(2)}) copy-start(bf16[4,4,32,320]{3,2,1,0:T(8,128)(2,1)S(1)} %fusion.18) | copy-start | bytes 983044
  268.5 1.1 copy-start.13
  298.1 7.4 %copy-start.1 = (bf16[4,4,32,6,32]{4,3,2,1,0:T(8,128)(2,1)S(1)}, bf16[4,4,32,6,32]{4,3,2,1,0:T(8,128)(2,1)}, u32[]{:S(2)}) copy-start(bf16[4,4,32,6,32]{4,3,2,1,0:T(8,128)(2,1)} %reshape.438) | copy-start | bytes 589828
  299.5 22.1 %all-to-all-start.5 = ((f32[64,1,2048]{2,1,0:T(1,128)}), f32[64,1,2048]{2,1,0:T(1,128)S(1)}, u32[]{:S(2)}, u32[]{:S(2)}) async-start(f32[64,1,2048]{2,1,0:T(1,128)} %broadcast_in_dim.119), calls=%async_computation.5 | async-start | bytes 1048576 | tf_op jit(solution)/shard_map/all_to_all | solution.py:34
  307.4 1.2 slice-start
  310.9 1.2 copy-start.10
  313.2 2.5 copy-start.21
  318.6 11.7 %copy-start.22 = (pred[256]{0:T(512)(128)(4,1)S(1)}, pred[256]{0:T(512)(128)(4,1)}, u32[]{:S(2)}) copy-start(pred[256]{0:T(512)(128)(4,1)} %get-tuple-element.27) | copy-start | bytes 772
  318.6 12.8 %copy-start.8 = (bf16[4,4,32,3,32]{4,3,2,1,0:T(4,128)(2,1)S(1)}, bf16[4,4,32,3,32]{4,3,2,1,0:T(4,128)(2,1)}, u32[]{:S(2)}) copy-start(bf16[4,4,32,3,32]{4,3,2,1,0:T(4,128)(2,1)} %get-tuple-element.35) | copy-start | bytes 294916
  321.6 0.8 copy-start.5
  322.4 107.8 %all-to-all-start.6 = ((bf16[64,32,1024]{2,1,0:T(8,128)(2,1)}), bf16[64,32,1024]{2,1,0:T(8,128)(2,1)}, u32[]{:S(2)}, u32[]{:S(2)}) async-start(bf16[64,32,1024]{2,1,0:T(8,128)(2,1)} %scatter_fusion), calls=%async_computation.6 | async-start | bytes 8388608 | tf_op jit(solution)/shard_map/all_to_all | solution.py:200
  331.9 3.0 copy-start.14
  333.3 1.8 copy-start.3
  335.1 1.0 copy-start.7
  336.4 112.2 %collective-permute-start.3 = (bf16[128,512]{1,0:T(8,128)(2,1)S(1)}, bf16[128,512]{1,0:T(8,128)(2,1)S(1)}, u32[]{:S(2)}, u32[]{:S(2)}) collective-permute-start(bf16[128,512]{1,0:T(8,128)(2,1)S(1)} %bitcast.266), channel_id=1, source_target_pairs={{0,0},{2,128},{4,256},{6,384},{128,2},{130,130},{132,258},{134,386... | collective-permute-start | bytes 393224 | tf_op jit(solution)/shard_map/ppermute | solution.py:48
  342.7 70.0 %collective-permute-start.4 = (bf16[32,1024]{1,0:T(8,128)(2,1)S(1)}, bf16[32,1024]{1,0:T(8,128)(2,1)S(1)}, u32[]{:S(2)}, u32[]{:S(2)}) collective-permute-start(bf16[32,1024]{1,0:T(8,128)(2,1)S(1)} %get-tuple-element.39), channel_id=1, source_target_pairs={{0,8},{8,16},{16,24},{24,32},{32,40},{40,48},{48,56},{56,64},{64,7... | collective-permute-start | bytes 196616 | tf_op jit(solution)/shard_map/ppermute | solution.py:20
  346.1 66.6 %collective-permute-start.5 = (bf16[32,1024]{1,0:T(8,128)(2,1)S(1)}, bf16[32,1024]{1,0:T(8,128)(2,1)S(1)}, u32[]{:S(2)}, u32[]{:S(2)}) collective-permute-start(bf16[32,1024]{1,0:T(8,128)(2,1)S(1)} %get-tuple-element.40), channel_id=1, source_target_pairs={{8,0},{16,8},{24,16},{32,24},{40,32},{48,40},{56,48},{64,56},{72,6... | collective-permute-start | bytes 196616 | tf_op jit(solution)/shard_map/ppermute | solution.py:21
  353.5 60.9 %copy-start.6 = (f32[64,1,2048]{2,1,0:T(1,128)S(1)}, f32[64,1,2048]{2,1,0:T(1,128)}, u32[]{:S(2)}) copy-start(f32[64,1,2048]{2,1,0:T(1,128)} %copy-done.5) | copy-start | bytes 1572868
  413.2 17.0 %copy-start.24 = (s32[64]{0:T(128)S(1)}, s32[64]{0:T(128)}, u32[]{:S(2)}) copy-start(s32[64]{0:T(128)} %copy-done.23) | copy-start | bytes 772
  415.8 21.1 %copy-start.17 = (pred[4]{0:T(512)(128)(4,1)S(1)}, pred[4]{0:T(512)(128)(4,1)}, u32[]{:S(2)}) copy-start(pred[4]{0:T(512)(128)(4,1)} %copy-done.16) | copy-start | bytes 16
  415.8 21.1 %copy-start.19 = (s32[4]{0:T(128)S(1)}, s32[4]{0:T(128)}, u32[]{:S(2)}) copy-start(s32[4]{0:T(128)} %copy-done.18) | copy-start | bytes 52
  438.0 40.3 %collective-permute-start.6 = (bf16[128,512]{1,0:T(8,128)(2,1)S(1)}, bf16[128,512]{1,0:T(8,128)(2,1)S(1)}, u32[]{:S(2)}, u32[]{:S(2)}) collective-permute-start(bf16[128,512]{1,0:T(8,128)(2,1)S(1)} %bitcast.268), channel_id=1, source_target_pairs={{0,0},{2,128},{4,256},{6,384},{128,2},{130,130},{132,258},{134,386... | collective-permute-start | bytes 393224 | tf_op jit(solution)/shard_map/ppermute | solution.py:48
  446.2 33.5 %collective-permute-start.7 = (bf16[128,512]{1,0:T(8,128)(2,1)S(1)}, bf16[128,512]{1,0:T(8,128)(2,1)S(1)}, u32[]{:S(2)}, u32[]{:S(2)}) collective-permute-start(bf16[128,512]{1,0:T(8,128)(2,1)S(1)} %bitcast.267), channel_id=1, source_target_pairs={{0,0},{2,128},{4,256},{6,384},{128,2},{130,130},{132,258},{134,386... | collective-permute-start | bytes 393224 | tf_op jit(solution)/shard_map/ppermute | solution.py:48

commit v3 on v2

--- a/solution.py
+++ b/solution.py
@@ -81,7 +81,6 @@
     global_offset = global_blocks % blocks_here
     owned = jnp.take(kv_blocks, global_offset, axis=0)
     owned = jnp.where((global_owner == my_index)[:, None, None], owned, jnp.zeros_like(owned))
-    global_kv = all_sum(owned, SEQ_AXES)
     entry_table = random_blocks.reshape(devices, entries)
     table_owner = entry_table // blocks_here
     table_offset = entry_table % blocks_here
@@ -99,7 +98,14 @@
     served_block = jnp.sum(jnp.where(served, table_offset[:, :, None], 0), axis=1)[range_at].reshape(-1)
     served_used = jnp.any(served, axis=1)[range_at].reshape(-1)
     outgoing = jnp.take(kv_blocks, served_block, axis=0)
+    owned_parts = owned.reshape(devices, -1, 2 * head_cols)
+    slot_rows = capacity * BS
+    outgoing = outgoing.reshape(devices, slot_rows, 2 * head_cols)
+    outgoing = jnp.concatenate([outgoing, owned_parts], axis=1)
     incoming = lax.all_to_all(outgoing, SEQ_AXES, split_axis=0, concat_axis=0, tiled=True)
+    global_chunk = jnp.sum(incoming[:, slot_rows:].astype(jnp.float32), axis=0)
+    global_kv = chunk_share(global_chunk, SEQ_AXES, owned.shape, owned.dtype)
+    incoming = incoming[:, :slot_rows].reshape(devices * capacity, BS, 2 * head_cols)
     fetched = jnp.take(incoming, my_target, axis=0).reshape(blocks_here, NR, BS, 2 * head_cols)
     near_kv = jnp.concatenate([window, fetched], axis=1)
     near_groups = 3 + NR
@@ -234,7 +240,8 @@
     )
     key_grad = own_grad[..., :head_cols].astype(jnp.bfloat16).reshape(tokens, head_cols)
     value_grad = own_grad[..., head_cols:].astype(jnp.bfloat16).reshape(tokens, head_cols)
-    return tuple(swap_places(out) for out in (query_grad, key_grad, value_grad))
+    outs = swap_places(jnp.stack([query_grad, key_grad, value_grad]))
+    return outs[0], outs[1], outs[2]
 
 
 def solution(mesh):

time: 491 us -> 513 us (1.045)
  the two profiles are of different devices: /device:TPU:2 before, /device:TPU:27 now
where the time goes in v3:
time: 513 us; the launch traced here: 507 us
  waiting for transfers between devices  311 us (61%)
  starting transfers between devices  72.9 us (14%)
  local copies, waits for them, and re-layouts  62.7 us (12%)
  blocking collectives  22.5 us (4%)
  matrix products  20.5 us (4%)
  other arithmetic  15.8 us (3%)
    ppermute x2, waiting for transfers between devices, with_halo(): before = lax.ppermute(x[length - width:], axis, up)  130 us
    ppermute x2, waiting for transfers between devices, swap_places(): return lax.ppermute(x, SWAP_AXES, pairs)  121 us
    all_to_all x1, waiting for transfers between devices, per_device(): lax.all_to_all(outgoing, SEQ_AXES, split_axis=0, concat_axis=0, tiled=True)  30.6 us
    all_to_all x1, waiting for transfers between devices, per_device(): lax.all_to_all(back_rows, SEQ_AXES, split_axis=0, concat_axis=0, tiled=True)  23.9 us
    all_to_all x1, blocking collectives, chunk_sum(): lax.all_to_all(x.reshape(peers, -1), axis, split_axis=0, concat_axis=0, t...  22.5 us
    all_to_all x2, starting transfers between devices, chunk_share(): lax.all_to_all(copies, axis, split_axis=0, concat_axis=0, tiled=True)  18.7 us
    ppermute x2, starting transfers between devices, swap_places(): return lax.ppermute(x, SWAP_AXES, pairs)  15.2 us
    all_to_all x1, starting transfers between devices, per_device(): lax.all_to_all(outgoing, SEQ_AXES, split_axis=0, concat_axis=0, tiled=True)  12.6 us
  transfers between devices with their start and end apart: 11, of which 7 were waited for; matrix products, arithmetic and copies ran while one was open for 10% of the time, Pallas kernels for 0%

profile of v3, /device:TPU:27, one launch (start us, length us, event | category | flops | bytes accessed | tf_op | source)
XLA Modules:
  0.0 506.9 jit_solution(11258331849461578765)
XLA Ops:
  0.7 1.0 copy.407
  1.6 0.9 copy.408
  2.6 0.9 copy.409
  3.5 0.9 copy.410
  4.6 1.0 copy.286
  5.5 5.1 %all-to-all-start = ((bf16[16,4,8,512]{3,0,1,2:T(8,128)(2,1)}), bf16[16,4,8,512]{3,0,1,2:T(8,128)(2,1)S(1)}, u32[]{:S(2)}, u32[]{:S(2)}) async-start(bf16[16,4,8,512]{3,0,1,2:T(8,128)(2,1)} %copy.286), calls=%async_computation | async-start | bytes 1048576 | tf_op jit(solution)/shard_map/all_to_all | solution.py:56
  13.9 5.2 %all-to-all-done = bf16[16,4,8,512]{3,0,1,2:T(8,128)(2,1)S(1)} async-done(((bf16[16,4,8,512]{3,0,1,2:T(8,128)(2,1)}), bf16[16,4,8,512]{3,0,1,2:T(8,128)(2,1)S(1)}, u32[]{:S(2)}, u32[]{:S(2)}) %all-to-all-start) | async-done | bytes 524320 | tf_op jit(solution)/shard_map/all_to_all | solution.py:56
  19.1 9.7 %collective-permute-start = (bf16[128,4,1,512]{3,0,1,2:T(8,128)(2,1)S(1)}, bf16[128,4,1,512]{3,0,1,2:T(8,128)(2,1)S(1)}, u32[]{:S(2)}, u32[]{:S(2)}) collective-permute-start(bf16[128,4,1,512]{3,0,1,2:T(8,128)(2,1)S(1)} %bitcast.256), channel_id=1, source_target_pairs={{0,0},{2,128},{4,256},{6,384},{128,2},{130,130},{132,258},{134,386... | collective-permute-start | bytes 1572872 | tf_op jit(solution)/shard_map/ppermute | solution.py:48
  28.8 67.5 %collective-permute-done = bf16[128,4,1,512]{3,0,1,2:T(8,128)(2,1)S(1)} collective-permute-done((bf16[128,4,1,512]{3,0,1,2:T(8,128)(2,1)S(1)}, bf16[128,4,1,512]{3,0,1,2:T(8,128)(2,1)S(1)}, u32[]{:S(2)}, u32[]{:S(2)}) %collective-permute-start) | collective-permute-done | bytes 524320 | tf_op jit(solution)/shard_map/ppermute | solution.py:48
  97.2 2.8 gather_fusion.2
  100.0 2.6 broadcast_select_fusion
  103.0 3.2 pad_maximum_fusion
  106.2 12.6 %all-to-all-start.1 = ((bf16[64,34,1024]{2,1,0:T(8,128)(2,1)}), bf16[64,34,1024]{2,1,0:T(8,128)(2,1)}, u32[]{:S(2)}, u32[]{:S(2)}) async-start(bf16[64,34,1024]{2,1,0:T(8,128)(2,1)} %pad_maximum_fusion), calls=%async_computation.1 | async-start | bytes 10485760 | tf_op jit(solution)/shard_map/all_to_all | solution.py:105
  120.9 3.1 collective-permute-start.1
  123.9 2.2 collective-permute-start.2
  126.2 77.6 %collective-permute-done.1 = bf16[32,1024]{1,0:T(8,128)(2,1)S(1)} collective-permute-done((bf16[32,1024]{1,0:T(8,128)(2,1)S(1)}, bf16[32,1024]{1,0:T(8,128)(2,1)S(1)}, u32[]{:S(2)}, u32[]{:S(2)}) %collective-permute-start.1) | collective-permute-done | bytes 65568 | tf_op jit(solution)/shard_map/ppermute | solution.py:20
  203.9 30.6 %all-to-all-done.1 = bf16[64,34,1024]{2,1,0:T(8,128)(2,1)} async-done(((bf16[64,34,1024]{2,1,0:T(8,128)(2,1)}), bf16[64,34,1024]{2,1,0:T(8,128)(2,1)}, u32[]{:S(2)}, u32[]{:S(2)}) %all-to-all-start.1) | async-done | bytes 4456480 | tf_op jit(solution)/shard_map/all_to_all | solution.py:105
  234.5 1.5 slice_reduce_fusion
  236.8 9.4 %all-to-all-start.2 = ((bf16[64,2,1024]{2,1,0:T(2,128)(2,1)}), bf16[64,2,1024]{2,1,0:T(2,128)(2,1)}, u32[]{:S(2)}, u32[]{:S(2)}) async-start(bf16[64,2,1024]{2,1,0:T(2,128)(2,1)} %broadcast_in_dim.129), calls=%async_computation.2 | async-start | bytes 524288 | tf_op jit(solution)/shard_map/all_to_all | solution.py:34
  246.2 5.0 slice.209
  251.3 2.8 gather_fusion.4
  254.4 1.2 slice_bitcast_fusion
  255.6 1.3 fusion.13
  256.9 1.2 copy.306
  258.6 2.4 fusion.11
  261.0 1.2 copy.312
  262.6 1.0 reshape.383
  268.0 1.0 convolution_bitcast_fusion.2
  269.0 1.0 convolution_bitcast_fusion.5
  270.0 1.7 reshape.390
  271.7 1.1 reshape.388
  272.8 1.3 convolution_bitcast_fusion
  274.1 2.6 copy.315
  276.7 2.4 reshape.389
  279.1 1.5 multiply_reduce_fusion
  280.6 1.5 fusion.18
  283.5 22.5 %all_to_all.49 = f32[64,1,2048]{2,1,0:T(1,128)S(1)} all-to-all(f32[64,1,2048]{2,1,0:T(1,128)S(1)} %all_to_all.42), channel_id=1, replica_groups=mesh['zh'=4,'zl'=4,'y'=4,'x'=4,'core'=2] {'zl','y','x'}, dimensions={0} | all-to-all | bytes 1048576 | tf_op jit(solution)/shard_map/all_to_all | solution.py:27
  306.4 1.1 broadcast_in_dim.131
  307.5 9.2 %all-to-all-start.4 = ((f32[64,1,2048]{2,1,0:T(1,128)}), f32[64,1,2048]{2,1,0:T(1,128)S(1)}, u32[]{:S(2)}, u32[]{:S(2)}) async-start(f32[64,1,2048]{2,1,0:T(1,128)} %broadcast_in_dim.131), calls=%async_computation.4 | async-start | bytes 1048576 | tf_op jit(solution)/shard_map/all_to_all | solution.py:34
  317.2 1.2 fusion.83
  318.4 1.0 copy.391
  319.4 1.2 fusion.53
  320.9 0.9 concatenate.90
  321.8 2.9 fusion.82
  324.7 1.0 copy.392
  325.6 1.2 fusion.57
  327.2 0.9 concatenate.91
  328.1 1.2 pad_maximum_fusion.2
  329.3 2.5 broadcast_in_dim.133
  331.8 2.8 scatter_fusion
  335.4 10.8 %all-to-all-start.5 = ((bf16[64,32,1024]{2,1,0:T(8,128)(2,1)}), bf16[64,32,1024]{2,1,0:T(8,128)(2,1)}, u32[]{:S(2)}, u32[]{:S(2)}) async-start(bf16[64,32,1024]{2,1,0:T(8,128)(2,1)} %scatter_fusion), calls=%async_computation.5 | async-start | bytes 8388608 | tf_op jit(solution)/shard_map/all_to_all | solution.py:206
  348.7 1.3 copy.389
  350.2 1.4 copy.381
  351.7 1.4 reshape.493
  353.4 3.1 collective-permute-start.3
  356.5 2.2 collective-permute-start.4
  359.8 52.4 %collective-permute-done.3 = bf16[32,1024]{1,0:T(8,128)(2,1)S(1)} collective-permute-done((bf16[32,1024]{1,0:T(8,128)(2,1)S(1)}, bf16[32,1024]{1,0:T(8,128)(2,1)S(1)}, u32[]{:S(2)}, u32[]{:S(2)}) %collective-permute-start.3) | collective-permute-done | bytes 65568 | tf_op jit(solution)/shard_map/ppermute | solution.py:20
  412.8 1.1 scatter-add.9
  413.9 1.2 reduce.15
  415.3 23.9 %all-to-all-done.5 = bf16[64,32,1024]{2,1,0:T(8,128)(2,1)} async-done(((bf16[64,32,1024]{2,1,0:T(8,128)(2,1)}), bf16[64,32,1024]{2,1,0:T(8,128)(2,1)}, u32[]{:S(2)}, u32[]{:S(2)}) %all-to-all-start.5) | async-done | bytes 4194336 | tf_op jit(solution)/shard_map/all_to_all | solution.py:206
  439.2 6.7 %fusion = f32[4,32,1024]{2,0,1:T(4,128)S(1)} fusion(bf16[64,32,1024]{2,1,0:T(8,128)(2,1)} %all-to-all-done.5, s32[64]{0:T(128)S(1)} %copy-done.19, pred[64]{0:T(512)(128)(4,1)S(1)} %gather_fusion.5), kind=kOutput, calls=%fused_computation.8 | convolution fusion | flops 16777728 | bytes 4718912 | tf_op jit(solution)/shard_map/jr,rkc->jkc/dot_general | solution.py:238
  445.9 1.0 fusion.3
  447.1 5.5 %collective-permute-start.5 = (bf16[3,128,512]{2,1,0:T(8,128)(2,1)S(1)}, bf16[3,128,512]{2,1,0:T(8,128)(2,1)S(1)}, u32[]{:S(2)}, u32[]{:S(2)}) collective-permute-start(bf16[3,128,512]{2,1,0:T(8,128)(2,1)S(1)} %pad_maximum_fusion.5), channel_id=1, source_target_pairs={{0,0},{2,128},{4,256},{6,384},{128,2},{130,130},{132,258},{134,386... | collective-permute-start | bytes 1179656 | tf_op jit(solution)/shard_map/ppermute | solution.py:48
  452.6 53.4 %collective-permute-done.5 = bf16[3,128,512]{2,1,0:T(8,128)(2,1)S(1)} collective-permute-done((bf16[3,128,512]{2,1,0:T(8,128)(2,1)S(1)}, bf16[3,128,512]{2,1,0:T(8,128)(2,1)S(1)}, u32[]{:S(2)}, u32[]{:S(2)}) %collective-permute-start.5) | collective-permute-done | bytes 393248 | tf_op jit(solution)/shard_map/ppermute | solution.py:48
  (163 shorter events, 22.0 us)
Async XLA Ops:
  0.6 12.4 %copy-start.21 = (s32[64]{0:T(128)S(1)}, s32[64]{0:T(128)}, u32[]{:S(2)}) copy-start(s32[64]{0:T(128)} %constant.200) | copy-start | bytes 772
  0.6 10.0 %copy-start.10 = (s32[256,3]{0,1:T(4,128)S(1)}, s32[256,3]{0,1:T(4,128)}, u32[]{:S(2)}) copy-start(s32[256,3]{0,1:T(4,128)} %param.18) | copy-start | bytes 9220
  0.7 11.9 %copy-start.20 = (s32[4]{0:T(128)S(1)}, s32[4]{0:T(128)}, u32[]{:S(2)}) copy-start(s32[4]{0:T(128)} %param.19) | copy-start | bytes 52
  5.5 13.5 %all-to-all-start = ((bf16[16,4,8,512]{3,0,1,2:T(8,128)(2,1)}), bf16[16,4,8,512]{3,0,1,2:T(8,128)(2,1)S(1)}, u32[]{:S(2)}, u32[]{:S(2)}) async-start(bf16[16,4,8,512]{3,0,1,2:T(8,128)(2,1)} %copy.286), calls=%async_computation | async-start | bytes 1048576 | tf_op jit(solution)/shard_map/all_to_all | solution.py:56
  12.6 83.9 %copy-start.11 = (s32[4]{0:T(128)}, s32[4]{0:T(128)S(1)}, u32[]{:S(2)}) copy-start(s32[4]{0:T(128)S(1)} %get-tuple-element.30) | copy-start | bytes 52
  12.6 83.9 %copy-start.13 = (pred[4]{0:T(512)(128)(4,1)}, pred[4]{0:T(512)(128)(4,1)S(1)}, u32[]{:S(2)}) copy-start(pred[4]{0:T(512)(128)(4,1)S(1)} %get-tuple-element.60) | copy-start | bytes 16
  13.8 82.6 %copy-start.18 = (s32[64]{0:T(128)}, s32[64]{0:T(128)S(1)}, u32[]{:S(2)}) copy-start(s32[64]{0:T(128)S(1)} %gather_fusion.1) | copy-start | bytes 772
  19.1 77.3 %collective-permute-start = (bf16[128,4,1,512]{3,0,1,2:T(8,128)(2,1)S(1)}, bf16[128,4,1,512]{3,0,1,2:T(8,128)(2,1)S(1)}, u32[]{:S(2)}, u32[]{:S(2)}) collective-permute-start(bf16[128,4,1,512]{3,0,1,2:T(8,128)(2,1)S(1)} %bitcast.256), channel_id=1, source_target_pairs={{0,0},{2,128},{4,256},{6,384},{128,2},{130,130},{132,258},{134,386... | collective-permute-start | bytes 1572872 | tf_op jit(solution)/shard_map/ppermute | solution.py:48
  106.2 12.8 %copy-start = (s32[64]{0:T(128)S(1)}, s32[64]{0:T(128)}, u32[]{:S(2)}) copy-start(s32[64]{0:T(128)} %constant.188.clone) | copy-start | bytes 772
  106.2 128.2 %all-to-all-start.1 = ((bf16[64,34,1024]{2,1,0:T(8,128)(2,1)}), bf16[64,34,1024]{2,1,0:T(8,128)(2,1)}, u32[]{:S(2)}, u32[]{:S(2)}) async-start(bf16[64,34,1024]{2,1,0:T(8,128)(2,1)} %pad_maximum_fusion), calls=%async_computation.1 | async-start | bytes 10485760 | tf_op jit(solution)/shard_map/all_to_all | solution.py:105
  120.3 0.5 copy-start.16
  120.9 83.0 %collective-permute-start.1 = (bf16[32,1024]{1,0:T(8,128)(2,1)S(1)}, bf16[32,1024]{1,0:T(8,128)(2,1)S(1)}, u32[]{:S(2)}, u32[]{:S(2)}) collective-permute-start(bf16[32,1024]{1,0:T(8,128)(2,1)S(1)} %get-tuple-element.58), channel_id=1, source_target_pairs={{0,8},{8,16},{16,24},{24,32},{32,40},{40,48},{48,56},{56,64},{64,7... | collective-permute-start | bytes 196616 | tf_op jit(solution)/shard_map/ppermute | solution.py:20
  123.9 79.9 %collective-permute-start.2 = (bf16[32,1024]{1,0:T(8,128)(2,1)S(1)}, bf16[32,1024]{1,0:T(8,128)(2,1)S(1)}, u32[]{:S(2)}, u32[]{:S(2)}) collective-permute-start(bf16[32,1024]{1,0:T(8,128)(2,1)S(1)} %get-tuple-element.59), channel_id=1, source_target_pairs={{8,0},{16,8},{24,16},{32,24},{40,32},{48,40},{56,48},{64,56},{72,6... | collective-permute-start | bytes 196616 | tf_op jit(solution)/shard_map/ppermute | solution.py:21
  236.8 25.8 %all-to-all-start.2 = ((bf16[64,2,1024]{2,1,0:T(2,128)(2,1)}), bf16[64,2,1024]{2,1,0:T(2,128)(2,1)}, u32[]{:S(2)}, u32[]{:S(2)}) async-start(bf16[64,2,1024]{2,1,0:T(2,128)(2,1)} %broadcast_in_dim.129), calls=%async_computation.2 | async-start | bytes 524288 | tf_op jit(solution)/shard_map/all_to_all | solution.py:34
  255.6 1.3 copy-start.2
  268.0 11.1 %copy-start.4 = (bf16[4,6,4,4,8,128]{5,4,3,2,1,0:T(8,128)(2,1)S(1)}, bf16[4,6,4,4,8,128]{5,4,3,2,1,0:T(8,128)(2,1)}, u32[]{:S(2)}) copy-start(bf16[4,6,4,4,8,128]{5,4,3,2,1,0:T(8,128)(2,1)} %get-tuple-element.33) | copy-start | bytes 2359300
  271.7 10.4 %copy-start.1 = (bf16[4,4,32,6,32]{4,3,2,1,0:T(8,128)(2,1)}, bf16[4,4,32,6,32]{4,3,2,1,0:T(8,128)(2,1)S(1)}, u32[]{:S(2)}) copy-start(bf16[4,4,32,6,32]{4,3,2,1,0:T(8,128)(2,1)S(1)} %reshape.390) | copy-start | bytes 589828
  280.6 2.2 copy-start.8
  307.5 27.2 %all-to-all-start.4 = ((f32[64,1,2048]{2,1,0:T(1,128)}), f32[64,1,2048]{2,1,0:T(1,128)S(1)}, u32[]{:S(2)}, u32[]{:S(2)}) async-start(f32[64,1,2048]{2,1,0:T(1,128)} %broadcast_in_dim.131), calls=%async_computation.4 | async-start | bytes 1048576 | tf_op jit(solution)/shard_map/all_to_all | solution.py:34
  326.9 4.9 copy-start.17
  334.6 11.6 %copy-start.15 = (pred[256]{0:T(512)(128)(4,1)S(1)}, pred[256]{0:T(512)(128)(4,1)}, u32[]{:S(2)}) copy-start(pred[256]{0:T(512)(128)(4,1)} %get-tuple-element.27) | copy-start | bytes 772
  334.6 12.6 %copy-start.7 = (bf16[4,4,32,3,32]{4,3,2,1,0:T(4,128)(2,1)S(1)}, bf16[4,4,32,3,32]{4,3,2,1,0:T(4,128)(2,1)}, u32[]{:S(2)}) copy-start(bf16[4,4,32,3,32]{4,3,2,1,0:T(4,128)(2,1)} %get-tuple-element.37) | copy-start | bytes 294916
  334.6 0.8 copy-start.5
  335.4 103.8 %all-to-all-start.5 = ((bf16[64,32,1024]{2,1,0:T(8,128)(2,1)}), bf16[64,32,1024]{2,1,0:T(8,128)(2,1)}, u32[]{:S(2)}, u32[]{:S(2)}) async-start(bf16[64,32,1024]{2,1,0:T(8,128)(2,1)} %scatter_fusion), calls=%async_computation.5 | async-start | bytes 8388608 | tf_op jit(solution)/shard_map/all_to_all | solution.py:206
  350.2 8.5 %copy-start.9 = (bf16[4,4,4,8,128]{4,3,2,1,0:T(8,128)(2,1)S(1)}, bf16[4,4,4,8,128]{4,3,2,1,0:T(8,128)(2,1)}, u32[]{:S(2)}) copy-start(bf16[4,4,4,8,128]{4,3,2,1,0:T(8,128)(2,1)} %get-tuple-element.50) | copy-start | bytes 393220
  353.1 6.0 %copy-start.3 = (bf16[4,6,4,4,8,128]{5,4,3,2,1,0:T(8,128)(2,1)S(1)}, bf16[4,6,4,4,8,128]{5,4,3,2,1,0:T(8,128)(2,1)}, u32[]{:S(2)}) copy-start(bf16[4,6,4,4,8,128]{5,4,3,2,1,0:T(8,128)(2,1)} %copy-done.2) | copy-start | bytes 2359300
  353.4 58.8 %collective-permute-start.3 = (bf16[32,1024]{1,0:T(8,128)(2,1)S(1)}, bf16[32,1024]{1,0:T(8,128)(2,1)S(1)}, u32[]{:S(2)}, u32[]{:S(2)}) collective-permute-start(bf16[32,1024]{1,0:T(8,128)(2,1)S(1)} %get-tuple-element.39), channel_id=1, source_target_pairs={{0,8},{8,16},{16,24},{24,32},{32,40},{40,48},{48,56},{56,64},{64,7... | collective-permute-start | bytes 196616 | tf_op jit(solution)/shard_map/ppermute | solution.py:20
  356.5 55.7 %collective-permute-start.4 = (bf16[32,1024]{1,0:T(8,128)(2,1)S(1)}, bf16[32,1024]{1,0:T(8,128)(2,1)S(1)}, u32[]{:S(2)}, u32[]{:S(2)}) collective-permute-start(bf16[32,1024]{1,0:T(8,128)(2,1)S(1)} %get-tuple-element.40), channel_id=1, source_target_pairs={{8,0},{16,8},{24,16},{32,24},{40,32},{48,40},{56,48},{64,56},{72,6... | collective-permute-start | bytes 196616 | tf_op jit(solution)/shard_map/ppermute | solution.py:21
  359.1 54.8 %copy-start.6 = (f32[64,1,2048]{2,1,0:T(1,128)S(1)}, f32[64,1,2048]{2,1,0:T(1,128)}, u32[]{:S(2)}) copy-start(f32[64,1,2048]{2,1,0:T(1,128)} %copy-done.5) | copy-start | bytes 1572868
  359.6 79.6 %copy-start.19 = (s32[64]{0:T(128)S(1)}, s32[64]{0:T(128)}, u32[]{:S(2)}) copy-start(s32[64]{0:T(128)} %copy-done.18) | copy-start | bytes 772
  412.6 33.3 %copy-start.12 = (s32[4]{0:T(128)S(1)}, s32[4]{0:T(128)}, u32[]{:S(2)}) copy-start(s32[4]{0:T(128)} %copy-done.11) | copy-start | bytes 52
  412.6 33.3 %copy-start.14 = (pred[4]{0:T(512)(128)(4,1)S(1)}, pred[4]{0:T(512)(128)(4,1)}, u32[]{:S(2)}) copy-start(pred[4]{0:T(512)(128)(4,1)} %copy-done.13) | copy-start | bytes 16
  447.1 58.9 %collective-permute-start.5 = (bf16[3,128,512]{2,1,0:T(8,128)(2,1)S(1)}, bf16[3,128,512]{2,1,0:T(8,128)(2,1)S(1)}, u32[]{:S(2)}, u32[]{:S(2)}) collective-permute-start(bf16[3,128,512]{2,1,0:T(8,128)(2,1)S(1)} %pad_maximum_fusion.5), channel_id=1, source_target_pairs={{0,0},{2,128},{4,256},{6,384},{128,2},{130,130},{132,258},{134,386... | collective-permute-start | bytes 1179656 | tf_op jit(solution)/shard_map/ppermute | solution.py:48

commit v4 on v3

--- a/solution.py
+++ b/solution.py
@@ -100,12 +100,14 @@
     outgoing = jnp.take(kv_blocks, served_block, axis=0)
     owned_parts = owned.reshape(devices, -1, 2 * head_cols)
     slot_rows = capacity * BS
-    outgoing = outgoing.reshape(devices, slot_rows, 2 * head_cols)
-    outgoing = jnp.concatenate([outgoing, owned_parts], axis=1)
+    slot_size = slot_rows * 2 * head_cols
+    outgoing = jnp.concatenate(
+        [outgoing.reshape(devices, slot_size), owned_parts.reshape(devices, -1)], axis=1
+    )
     incoming = lax.all_to_all(outgoing, SEQ_AXES, split_axis=0, concat_axis=0, tiled=True)
-    global_chunk = jnp.sum(incoming[:, slot_rows:].astype(jnp.float32), axis=0)
+    global_chunk = jnp.sum(incoming[:, slot_size:].astype(jnp.float32), axis=0)
     global_kv = chunk_share(global_chunk, SEQ_AXES, owned.shape, owned.dtype)
-    incoming = incoming[:, :slot_rows].reshape(devices * capacity, BS, 2 * head_cols)
+    incoming = incoming[:, :slot_size].reshape(devices * capacity, BS, 2 * head_cols)
     fetched = jnp.take(incoming, my_target, axis=0).reshape(blocks_here, NR, BS, 2 * head_cols)
     near_kv = jnp.concatenate([window, fetched], axis=1)
     near_groups = 3 + NR

time: 513 us -> 544 us (1.060)
  the two profiles are of different devices: /device:TPU:27 before, /device:TPU:3 now
where the time goes in v4:
time: 544 us; the launch traced here: 535 us
  waiting for transfers between devices  288 us (53%)
  local copies, waits for them, and re-layouts  103 us (19%)
  starting transfers between devices  75.5 us (14%)
  blocking collectives  24.8 us (5%)
  other arithmetic  21.8 us (4%)
  matrix products  20.6 us (4%)
    ppermute x2, waiting for transfers between devices, swap_places(): return lax.ppermute(x, SWAP_AXES, pairs)  121 us
    ppermute x2, waiting for transfers between devices, with_halo(): before = lax.ppermute(x[length - width:], axis, up)  120 us
    unnamed x63, local copies, waits for them, and re-layouts  56.8 us
    all_to_all x1, blocking collectives, chunk_sum(): lax.all_to_all(x.reshape(peers, -1), axis, split_axis=0, concat_axis=0, t...  24.8 us
    all_to_all x1, waiting for transfers between devices, per_device(): lax.all_to_all(outgoing, SEQ_AXES, split_axis=0, concat_axis=0, tiled=True)  21.5 us
    all_to_all x1, waiting for transfers between devices, per_device(): lax.all_to_all(back_rows, SEQ_AXES, split_axis=0, concat_axis=0, tiled=True)  19.3 us
    ppermute x2, starting transfers between devices, with_halo(): after = lax.ppermute(x[:width], axis, down)  14.2 us
    all_to_all x2, starting transfers between devices, chunk_share(): lax.all_to_all(copies, axis, split_axis=0, concat_axis=0, tiled=True)  13.3 us
  transfers between devices with their start and end apart: 11, of which 7 were waited for; matrix products, arithmetic and copies ran while one was open for 8% of the time, Pallas kernels for 0%

profile of v4, /device:TPU:3, one launch (start us, length us, event | category | flops | bytes accessed | tf_op | source)
XLA Modules:
  0.0 535.0 jit_solution(2936729004295428902)
XLA Ops:
  2.6 0.9 copy.476
  4.5 1.0 copy.351
  5.5 9.6 %all-to-all-start = ((bf16[16,4,8,512]{3,0,1,2:T(8,128)(2,1)}), bf16[16,4,8,512]{3,0,1,2:T(8,128)(2,1)S(1)}, u32[]{:S(2)}, u32[]{:S(2)}) async-start(bf16[16,4,8,512]{3,0,1,2:T(8,128)(2,1)} %copy.351), calls=%async_computation | async-start | bytes 1048576 | tf_op jit(solution)/shard_map/all_to_all | solution.py:56
  18.0 5.5 %all-to-all-done = bf16[16,4,8,512]{3,0,1,2:T(8,128)(2,1)S(1)} async-done(((bf16[16,4,8,512]{3,0,1,2:T(8,128)(2,1)}), bf16[16,4,8,512]{3,0,1,2:T(8,128)(2,1)S(1)}, u32[]{:S(2)}, u32[]{:S(2)}) %all-to-all-start) | async-done | bytes 524320 | tf_op jit(solution)/shard_map/all_to_all | solution.py:56
  23.6 5.2 collective-permute-start
  28.8 69.8 %collective-permute-done = bf16[128,4,1,512]{3,0,1,2:T(8,128)(2,1)S(1)} collective-permute-done((bf16[128,4,1,512]{3,0,1,2:T(8,128)(2,1)S(1)}, bf16[128,4,1,512]{3,0,1,2:T(8,128)(2,1)S(1)}, u32[]{:S(2)}, u32[]{:S(2)}) %collective-permute-start) | collective-permute-done | bytes 524320 | tf_op jit(solution)/shard_map/ppermute | solution.py:48
  99.6 2.8 gather_fusion.2
  102.3 4.6 copy.478
  107.5 2.4 maximum_bitcast_fusion
  110.4 7.0 %reduce.19 = bf16[64,34816]{1,0:T(8,128)(2,1)} reduce(bf16[64,1,34816]{2,0,1:T(8,128)(2,1)} %maximum_bitcast_fusion, bf16[]{:T(256)} %broadcast.423), dimensions={1}, to_apply=%copy.366.reduce_sub_computation | reduce | bytes 8912898 | tf_op jit(solution)/shard_map/all_to_all | solution.py:107
  117.4 8.1 %reshape.518 = bf16[64,2,17408]{2,1,0:T(2,128)(2,1)} reshape(bf16[64,34816]{1,0:T(8,128)(2,1)} %reduce.19) | data formatting | bytes 8912896
  125.5 10.6 %all-to-all-start.1 = ((bf16[64,2,17408]{2,1,0:T(2,128)(2,1)}), bf16[64,2,17408]{2,1,0:T(2,128)(2,1)}, u32[]{:S(2)}, u32[]{:S(2)}) async-start(bf16[64,2,17408]{2,1,0:T(2,128)(2,1)} %reshape.518), calls=%async_computation.1 | async-start | bytes 8912896 | tf_op jit(solution)/shard_map/all_to_all | solution.py:107
  138.1 3.1 collective-permute-start.1
  141.2 7.2 %collective-permute-start.2 = (bf16[32,1024]{1,0:T(8,128)(2,1)S(1)}, bf16[32,1024]{1,0:T(8,128)(2,1)S(1)}, u32[]{:S(2)}, u32[]{:S(2)}) collective-permute-start(bf16[32,1024]{1,0:T(8,128)(2,1)S(1)} %get-tuple-element.59), channel_id=1, source_target_pairs={{8,0},{16,8},{24,16},{32,24},{40,32},{48,40},{56,48},{64,56},{72,6... | collective-permute-start | bytes 196616 | tf_op jit(solution)/shard_map/ppermute | solution.py:21
  148.5 66.5 %collective-permute-done.1 = bf16[32,1024]{1,0:T(8,128)(2,1)S(1)} collective-permute-done((bf16[32,1024]{1,0:T(8,128)(2,1)S(1)}, bf16[32,1024]{1,0:T(8,128)(2,1)S(1)}, u32[]{:S(2)}, u32[]{:S(2)}) %collective-permute-start.1) | collective-permute-done | bytes 65568 | tf_op jit(solution)/shard_map/ppermute | solution.py:20
  215.1 21.5 %all-to-all-done.1 = bf16[64,2,17408]{2,1,0:T(2,128)(2,1)} async-done(((bf16[64,2,17408]{2,1,0:T(2,128)(2,1)}), bf16[64,2,17408]{2,1,0:T(2,128)(2,1)}, u32[]{:S(2)}, u32[]{:S(2)}) %all-to-all-start.1) | async-done | bytes 4456480 | tf_op jit(solution)/shard_map/all_to_all | solution.py:107
  236.6 19.7 %reshape.519 = bf16[64,1,34816]{2,1,0:T(2,128)(2,1)} reshape(bf16[64,2,17408]{2,1,0:T(2,128)(2,1)} %all-to-all-done.1) | data formatting | bytes 8912896
  256.3 6.0 %copy.553 = bf16[64,1,34816]{2,0,1:T(8,128)(2,1)S(1)} copy(bf16[64,1,34816]{2,1,0:T(2,128)(2,1)} %reshape.519) | data formatting | bytes 8912896
  262.7 4.4 copy.479
  267.4 2.2 reduce.20
  270.5 6.4 %all-to-all-start.2 = ((bf16[64,2,1024]{2,1,0:T(2,128)(2,1)}), bf16[64,2,1024]{2,1,0:T(2,128)(2,1)}, u32[]{:S(2)}, u32[]{:S(2)}) async-start(bf16[64,2,1024]{2,1,0:T(2,128)(2,1)} %reshape.520), calls=%async_computation.2 | async-start | bytes 524288 | tf_op jit(solution)/shard_map/all_to_all | solution.py:34
  276.9 2.8 gather_fusion.4
  280.0 1.2 slice_bitcast_fusion
  281.2 1.3 fusion.13
  282.5 1.2 copy.372
  284.2 2.4 fusion.11
  286.6 1.2 copy.378
  288.2 2.1 reshape.521
  290.4 1.5 reduce.15
  296.3 1.0 convolution_bitcast_fusion.2
  297.3 1.0 convolution_bitcast_fusion.5
  298.3 2.0 reshape.407
  300.3 1.1 reshape.405
  301.4 1.3 convolution_bitcast_fusion
  302.7 2.6 copy.381
  305.3 2.4 reshape.406
  307.7 1.5 multiply_reduce_fusion
  309.2 1.5 fusion.18
  312.1 24.8 %all_to_all.57 = f32[64,1,2048]{2,1,0:T(1,128)S(1)} all-to-all(f32[64,1,2048]{2,1,0:T(1,128)S(1)} %all_to_all.50), channel_id=1, replica_groups=mesh['zh'=4,'zl'=4,'y'=4,'x'=4,'core'=2] {'zl','y','x'}, dimensions={0} | all-to-all | bytes 1048576 | tf_op jit(solution)/shard_map/all_to_all | solution.py:27
  337.3 1.1 broadcast_in_dim.119
  338.4 6.9 %all-to-all-start.4 = ((f32[64,1,2048]{2,1,0:T(1,128)}), f32[64,1,2048]{2,1,0:T(1,128)S(1)}, u32[]{:S(2)}, u32[]{:S(2)}) async-start(f32[64,1,2048]{2,1,0:T(1,128)} %broadcast_in_dim.119), calls=%async_computation.4 | async-start | bytes 1048576 | tf_op jit(solution)/shard_map/all_to_all | solution.py:34
  345.8 1.2 fusion.83
  347.0 1.0 copy.458
  348.0 1.2 fusion.53
  350.4 2.9 fusion.82
  353.3 1.0 copy.459
  354.3 1.2 fusion.57
  356.7 1.2 pad_maximum_fusion.1
  357.9 2.5 broadcast_in_dim.121
  360.4 2.9 scatter_fusion
  364.2 10.6 %all-to-all-start.5 = ((bf16[64,32,1024]{2,1,0:T(8,128)(2,1)}), bf16[64,32,1024]{2,1,0:T(8,128)(2,1)}, u32[]{:S(2)}, u32[]{:S(2)}) async-start(bf16[64,32,1024]{2,1,0:T(8,128)(2,1)} %scatter_fusion), calls=%async_computation.5 | async-start | bytes 8388608 | tf_op jit(solution)/shard_map/all_to_all | solution.py:208
  377.3 1.3 copy.456
  378.8 1.4 copy.447
  380.2 1.4 reshape.510
  382.0 3.1 collective-permute-start.3
  385.1 7.0 %collective-permute-start.4 = (bf16[32,1024]{1,0:T(8,128)(2,1)S(1)}, bf16[32,1024]{1,0:T(8,128)(2,1)S(1)}, u32[]{:S(2)}, u32[]{:S(2)}) collective-permute-start(bf16[32,1024]{1,0:T(8,128)(2,1)S(1)} %get-tuple-element.40), channel_id=1, source_target_pairs={{8,0},{16,8},{24,16},{32,24},{40,32},{48,40},{56,48},{64,56},{72,6... | collective-permute-start | bytes 196616 | tf_op jit(solution)/shard_map/ppermute | solution.py:21
  393.2 53.4 %collective-permute-done.3 = bf16[32,1024]{1,0:T(8,128)(2,1)S(1)} collective-permute-done((bf16[32,1024]{1,0:T(8,128)(2,1)S(1)}, bf16[32,1024]{1,0:T(8,128)(2,1)S(1)}, u32[]{:S(2)}, u32[]{:S(2)}) %collective-permute-start.3) | collective-permute-done | bytes 65568 | tf_op jit(solution)/shard_map/ppermute | solution.py:20
  447.2 1.1 scatter-add.9
  448.3 1.2 reduce.16
  449.6 19.3 %all-to-all-done.5 = bf16[64,32,1024]{2,1,0:T(8,128)(2,1)} async-done(((bf16[64,32,1024]{2,1,0:T(8,128)(2,1)}), bf16[64,32,1024]{2,1,0:T(8,128)(2,1)}, u32[]{:S(2)}, u32[]{:S(2)}) %all-to-all-start.5) | async-done | bytes 4194336 | tf_op jit(solution)/shard_map/all_to_all | solution.py:208
  468.9 6.7 %fusion = f32[4,32,1024]{2,0,1:T(4,128)S(1)} fusion(bf16[64,32,1024]{2,1,0:T(8,128)(2,1)} %all-to-all-done.5, s32[64]{0:T(128)S(1)} %copy-done.19, pred[64]{0:T(512)(128)(4,1)S(1)} %gather_fusion.5), kind=kOutput, calls=%fused_computation.9 | convolution fusion | flops 16777728 | bytes 4718912 | tf_op jit(solution)/shard_map/jr,rkc->jkc/dot_general | solution.py:240
  475.6 1.0 fusion.3
  476.8 5.7 %collective-permute-start.5 = (bf16[3,128,512]{2,1,0:T(8,128)(2,1)S(1)}, bf16[3,128,512]{2,1,0:T(8,128)(2,1)S(1)}, u32[]{:S(2)}, u32[]{:S(2)}) collective-permute-start(bf16[3,128,512]{2,1,0:T(8,128)(2,1)S(1)} %pad_maximum_fusion.4), channel_id=1, source_target_pairs={{0,0},{2,128},{4,256},{6,384},{128,2},{130,130},{132,258},{134,386... | collective-permute-start | bytes 1179656 | tf_op jit(solution)/shard_map/ppermute | solution.py:48
  482.5 51.5 %collective-permute-done.5 = bf16[3,128,512]{2,1,0:T(8,128)(2,1)S(1)} collective-permute-done((bf16[3,128,512]{2,1,0:T(8,128)(2,1)S(1)}, bf16[3,128,512]{2,1,0:T(8,128)(2,1)S(1)}, u32[]{:S(2)}, u32[]{:S(2)}) %collective-permute-start.5) | collective-permute-done | bytes 393248 | tf_op jit(solution)/shard_map/ppermute | solution.py:48
  (170 shorter events, 27.8 us)
Async XLA Ops:
  0.6 16.3 %copy-start.21 = (s32[64]{0:T(128)S(1)}, s32[64]{0:T(128)}, u32[]{:S(2)}) copy-start(s32[64]{0:T(128)} %constant.200) | copy-start | bytes 772
  0.6 14.5 %copy-start.10 = (s32[256,3]{0,1:T(4,128)S(1)}, s32[256,3]{0,1:T(4,128)}, u32[]{:S(2)}) copy-start(s32[256,3]{0,1:T(4,128)} %param.18) | copy-start | bytes 9220
  0.7 17.3 %copy-start.20 = (s32[4]{0:T(128)S(1)}, s32[4]{0:T(128)}, u32[]{:S(2)}) copy-start(s32[4]{0:T(128)} %param.19) | copy-start | bytes 52
  5.5 18.0 %all-to-all-start = ((bf16[16,4,8,512]{3,0,1,2:T(8,128)(2,1)}), bf16[16,4,8,512]{3,0,1,2:T(8,128)(2,1)S(1)}, u32[]{:S(2)}, u32[]{:S(2)}) async-start(bf16[16,4,8,512]{3,0,1,2:T(8,128)(2,1)} %copy.351), calls=%async_computation | async-start | bytes 1048576 | tf_op jit(solution)/shard_map/all_to_all | solution.py:56
  18.0 80.8 %copy-start.18 = (s32[64]{0:T(128)}, s32[64]{0:T(128)S(1)}, u32[]{:S(2)}) copy-start(s32[64]{0:T(128)S(1)} %gather_fusion.1) | copy-start | bytes 772
  18.0 10.8 %copy-start.13 = (s32[4]{0:T(128)}, s32[4]{0:T(128)S(1)}, u32[]{:S(2)}) copy-start(s32[4]{0:T(128)S(1)} %get-tuple-element.30) | copy-start | bytes 52
  18.0 84.3 %copy-start.11 = (pred[4]{0:T(512)(128)(4,1)}, pred[4]{0:T(512)(128)(4,1)S(1)}, u32[]{:S(2)}) copy-start(pred[4]{0:T(512)(128)(4,1)S(1)} %get-tuple-element.60) | copy-start | bytes 16
  23.6 75.1 %collective-permute-start = (bf16[128,4,1,512]{3,0,1,2:T(8,128)(2,1)S(1)}, bf16[128,4,1,512]{3,0,1,2:T(8,128)(2,1)S(1)}, u32[]{:S(2)}, u32[]{:S(2)}) collective-permute-start(bf16[128,4,1,512]{3,0,1,2:T(8,128)(2,1)S(1)} %bitcast.271), channel_id=1, source_target_pairs={{0,0},{2,128},{4,256},{6,384},{128,2},{130,130},{132,258},{134,386... | collective-permute-start | bytes 1572872 | tf_op jit(solution)/shard_map/ppermute | solution.py:48
  125.5 10.9 %copy-start = (s32[64]{0:T(128)S(1)}, s32[64]{0:T(128)}, u32[]{:S(2)}) copy-start(s32[64]{0:T(128)} %constant.188.clone) | copy-start | bytes 772
  125.5 111.1 %all-to-all-start.1 = ((bf16[64,2,17408]{2,1,0:T(2,128)(2,1)}), bf16[64,2,17408]{2,1,0:T(2,128)(2,1)}, u32[]{:S(2)}, u32[]{:S(2)}) async-start(bf16[64,2,17408]{2,1,0:T(2,128)(2,1)} %reshape.518), calls=%async_computation.1 | async-start | bytes 8912896 | tf_op jit(solution)/shard_map/all_to_all | solution.py:107
  137.6 0.5 copy-start.16
  138.1 76.9 %collective-permute-start.1 = (bf16[32,1024]{1,0:T(8,128)(2,1)S(1)}, bf16[32,1024]{1,0:T(8,128)(2,1)S(1)}, u32[]{:S(2)}, u32[]{:S(2)}) collective-permute-start(bf16[32,1024]{1,0:T(8,128)(2,1)S(1)} %get-tuple-element.58), channel_id=1, source_target_pairs={{0,8},{8,16},{16,24},{24,32},{32,40},{40,48},{48,56},{56,64},{64,7... | collective-permute-start | bytes 196616 | tf_op jit(solution)/shard_map/ppermute | solution.py:20
  141.2 73.8 %collective-permute-start.2 = (bf16[32,1024]{1,0:T(8,128)(2,1)S(1)}, bf16[32,1024]{1,0:T(8,128)(2,1)S(1)}, u32[]{:S(2)}, u32[]{:S(2)}) collective-permute-start(bf16[32,1024]{1,0:T(8,128)(2,1)S(1)} %get-tuple-element.59), channel_id=1, source_target_pairs={{8,0},{16,8},{24,16},{32,24},{40,32},{48,40},{56,48},{64,56},{72,6... | collective-permute-start | bytes 196616 | tf_op jit(solution)/shard_map/ppermute | solution.py:21
  270.5 17.7 %all-to-all-start.2 = ((bf16[64,2,1024]{2,1,0:T(2,128)(2,1)}), bf16[64,2,1024]{2,1,0:T(2,128)(2,1)}, u32[]{:S(2)}, u32[]{:S(2)}) async-start(bf16[64,2,1024]{2,1,0:T(2,128)(2,1)} %reshape.520), calls=%async_computation.2 | async-start | bytes 524288 | tf_op jit(solution)/shard_map/all_to_all | solution.py:34
  281.2 1.3 copy-start.2
  296.3 11.4 %copy-start.4 = (bf16[4,6,4,4,8,128]{5,4,3,2,1,0:T(8,128)(2,1)S(1)}, bf16[4,6,4,4,8,128]{5,4,3,2,1,0:T(8,128)(2,1)}, u32[]{:S(2)}) copy-start(bf16[4,6,4,4,8,128]{5,4,3,2,1,0:T(8,128)(2,1)} %get-tuple-element.33) | copy-start | bytes 2359300
  300.3 10.4 %copy-start.1 = (bf16[4,4,32,6,32]{4,3,2,1,0:T(8,128)(2,1)}, bf16[4,4,32,6,32]{4,3,2,1,0:T(8,128)(2,1)S(1)}, u32[]{:S(2)}) copy-start(bf16[4,4,32,6,32]{4,3,2,1,0:T(8,128)(2,1)S(1)} %reshape.407) | copy-start | bytes 589828
  309.2 2.2 copy-start.8
  338.4 25.0 %all-to-all-start.4 = ((f32[64,1,2048]{2,1,0:T(1,128)}), f32[64,1,2048]{2,1,0:T(1,128)S(1)}, u32[]{:S(2)}, u32[]{:S(2)}) async-start(f32[64,1,2048]{2,1,0:T(1,128)} %broadcast_in_dim.119), calls=%async_computation.4 | async-start | bytes 1048576 | tf_op jit(solution)/shard_map/all_to_all | solution.py:34
  355.5 4.9 copy-start.17
  363.3 11.5 %copy-start.15 = (pred[256]{0:T(512)(128)(4,1)S(1)}, pred[256]{0:T(512)(128)(4,1)}, u32[]{:S(2)}) copy-start(pred[256]{0:T(512)(128)(4,1)} %get-tuple-element.27) | copy-start | bytes 772
  363.3 12.5 %copy-start.7 = (bf16[4,4,32,3,32]{4,3,2,1,0:T(4,128)(2,1)S(1)}, bf16[4,4,32,3,32]{4,3,2,1,0:T(4,128)(2,1)}, u32[]{:S(2)}) copy-start(bf16[4,4,32,3,32]{4,3,2,1,0:T(4,128)(2,1)} %get-tuple-element.37) | copy-start | bytes 294916
  363.3 0.8 copy-start.5
  364.2 104.7 %all-to-all-start.5 = ((bf16[64,32,1024]{2,1,0:T(8,128)(2,1)}), bf16[64,32,1024]{2,1,0:T(8,128)(2,1)}, u32[]{:S(2)}, u32[]{:S(2)}) async-start(bf16[64,32,1024]{2,1,0:T(8,128)(2,1)} %scatter_fusion), calls=%async_computation.5 | async-start | bytes 8388608 | tf_op jit(solution)/shard_map/all_to_all | solution.py:208
  378.8 13.3 %copy-start.9 = (bf16[4,4,4,8,128]{4,3,2,1,0:T(8,128)(2,1)S(1)}, bf16[4,4,4,8,128]{4,3,2,1,0:T(8,128)(2,1)}, u32[]{:S(2)}) copy-start(bf16[4,4,4,8,128]{4,3,2,1,0:T(8,128)(2,1)} %get-tuple-element.50) | copy-start | bytes 393220
  381.7 10.8 %copy-start.3 = (bf16[4,6,4,4,8,128]{5,4,3,2,1,0:T(8,128)(2,1)S(1)}, bf16[4,6,4,4,8,128]{5,4,3,2,1,0:T(8,128)(2,1)}, u32[]{:S(2)}) copy-start(bf16[4,6,4,4,8,128]{5,4,3,2,1,0:T(8,128)(2,1)} %copy-done.2) | copy-start | bytes 2359300
  382.0 64.6 %collective-permute-start.3 = (bf16[32,1024]{1,0:T(8,128)(2,1)S(1)}, bf16[32,1024]{1,0:T(8,128)(2,1)S(1)}, u32[]{:S(2)}, u32[]{:S(2)}) collective-permute-start(bf16[32,1024]{1,0:T(8,128)(2,1)S(1)} %get-tuple-element.39), channel_id=1, source_target_pairs={{0,8},{8,16},{16,24},{24,32},{32,40},{40,48},{48,56},{56,64},{64,7... | collective-permute-start | bytes 196616 | tf_op jit(solution)/shard_map/ppermute | solution.py:20
  385.1 61.5 %collective-permute-start.4 = (bf16[32,1024]{1,0:T(8,128)(2,1)S(1)}, bf16[32,1024]{1,0:T(8,128)(2,1)S(1)}, u32[]{:S(2)}, u32[]{:S(2)}) collective-permute-start(bf16[32,1024]{1,0:T(8,128)(2,1)S(1)} %get-tuple-element.40), channel_id=1, source_target_pairs={{8,0},{16,8},{24,16},{32,24},{40,32},{48,40},{56,48},{64,56},{72,6... | collective-permute-start | bytes 196616 | tf_op jit(solution)/shard_map/ppermute | solution.py:21
  392.5 55.8 %copy-start.6 = (f32[64,1,2048]{2,1,0:T(1,128)S(1)}, f32[64,1,2048]{2,1,0:T(1,128)}, u32[]{:S(2)}) copy-start(f32[64,1,2048]{2,1,0:T(1,128)} %copy-done.5) | copy-start | bytes 1572868
  393.0 75.9 %copy-start.19 = (s32[64]{0:T(128)S(1)}, s32[64]{0:T(128)}, u32[]{:S(2)}) copy-start(s32[64]{0:T(128)} %copy-done.18) | copy-start | bytes 772
  447.0 28.6 %copy-start.12 = (pred[4]{0:T(512)(128)(4,1)S(1)}, pred[4]{0:T(512)(128)(4,1)}, u32[]{:S(2)}) copy-start(pred[4]{0:T(512)(128)(4,1)} %copy-done.11) | copy-start | bytes 16
  447.0 28.6 %copy-start.14 = (s32[4]{0:T(128)S(1)}, s32[4]{0:T(128)}, u32[]{:S(2)}) copy-start(s32[4]{0:T(128)} %copy-done.13) | copy-start | bytes 52
  476.8 57.3 %collective-permute-start.5 = (bf16[3,128,512]{2,1,0:T(8,128)(2,1)S(1)}, bf16[3,128,512]{2,1,0:T(8,128)(2,1)S(1)}, u32[]{:S(2)}, u32[]{:S(2)}) collective-permute-start(bf16[3,128,512]{2,1,0:T(8,128)(2,1)S(1)} %pad_maximum_fusion.4), channel_id=1, source_target_pairs={{0,0},{2,128},{4,256},{6,384},{128,2},{130,130},{132,258},{134,386... | collective-permute-start | bytes 1179656 | tf_op jit(solution)/shard_map/ppermute | solution.py:48

commit v5 on v2

--- a/solution.py
+++ b/solution.py
@@ -54,6 +54,12 @@
     stacked = jnp.stack([queries, key_states, value_states, out_grad], axis=1)
     stacked = stacked.reshape(rows_in, 4, groups, cols_in // groups)
     stacked = lax.all_to_all(stacked, ("x", "core"), split_axis=2, concat_axis=0, tiled=True)
+    home_index = lax.axis_index(("zh", "zl", "y"))
+    home_blocks = stacked.shape[0] // BS
+    home_kv = jnp.concatenate([stacked[:, 1, 0], stacked[:, 2, 0]], axis=1).reshape(home_blocks, BS, -1)
+    owned = jnp.take(home_kv, global_blocks % home_blocks, axis=0)
+    owned = jnp.where((global_blocks // home_blocks == home_index)[:, None, None], owned, jnp.zeros_like(owned))
+    global_chunk = swap_places(chunk_sum(owned, ("zh", "zl", "y")).astype(owned.dtype))
     stacked = swap_places(stacked)
     query_rows, key_rows, value_rows, grad_rows = (stacked[:, i, 0] for i in range(4))
     tokens = query_rows.shape[0]
@@ -79,9 +85,8 @@
     )
     global_owner = global_blocks // blocks_here
     global_offset = global_blocks % blocks_here
-    owned = jnp.take(kv_blocks, global_offset, axis=0)
-    owned = jnp.where((global_owner == my_index)[:, None, None], owned, jnp.zeros_like(owned))
-    global_kv = all_sum(owned, SEQ_AXES)
+    shared = chunk_share(global_chunk, SEQ_AXES, (devices,) + global_chunk.shape, owned.dtype)
+    global_kv = jnp.take(shared, slot_of, axis=0).reshape(owned.shape)
     entry_table = random_blocks.reshape(devices, entries)
     table_owner = entry_table // blocks_here
     table_offset = entry_table % blocks_here

time: 491 us -> 494 us (level)
  the two profiles are of different devices: /device:TPU:2 before, /device:TPU:3 now
where the time goes in v5:
time: 494 us; the launch traced here: 485 us
  waiting for transfers between devices  261 us (53%)
  starting transfers between devices  108 us (22%)
  local copies, waits for them, and re-layouts  54.7 us (11%)
  blocking collectives  25.8 us (5%)
  other arithmetic  17.1 us (3%)
  matrix products  16.4 us (3%)
    ppermute x2, waiting for transfers between devices, with_halo(): before = lax.ppermute(x[length - width:], axis, up)  114 us
    ppermute x5, waiting for transfers between devices, swap_places(): return lax.ppermute(x, SWAP_AXES, pairs)  94.6 us
    ppermute x5, starting transfers between devices, swap_places(): return lax.ppermute(x, SWAP_AXES, pairs)  32.8 us
    all_to_all x1, blocking collectives, chunk_sum(): lax.all_to_all(x.reshape(peers, -1), axis, split_axis=0, concat_axis=0, t...  25.8 us
    all_to_all x1, waiting for transfers between devices, per_device(): lax.all_to_all(outgoing, SEQ_AXES, split_axis=0, concat_axis=0, tiled=True)  18.1 us
    all_to_all x2, starting transfers between devices, chunk_share(): lax.all_to_all(copies, axis, split_axis=0, concat_axis=0, tiled=True)  15.2 us
    all_to_all x1, waiting for transfers between devices, per_device(): lax.all_to_all(back_rows, SEQ_AXES, split_axis=0, concat_axis=0, tiled=True)  14.8 us
    ppermute x2, starting transfers between devices, with_halo(): after = lax.ppermute(x[:width], axis, down)  14.2 us
  transfers between devices with their start and end apart: 15, of which 11 were waited for; matrix products, arithmetic and copies ran while one was open for 11% of the time, Pallas kernels for 0%

profile of v5, /device:TPU:3, one launch (start us, length us, event | category | flops | bytes accessed | tf_op | source)
XLA Modules:
  0.0 485.2 jit_solution(3545879367535017040)
XLA Ops:
  0.6 0.9 copy.475
  1.6 0.9 copy.476
  2.5 0.9 copy.477
  3.5 0.9 copy.478
  4.5 1.0 copy.352
  5.5 9.6 %all-to-all-start = ((bf16[16,4,8,512]{3,0,1,2:T(8,128)(2,1)}), bf16[16,4,8,512]{3,0,1,2:T(8,128)(2,1)S(1)}, u32[]{:S(2)}, u32[]{:S(2)}) async-start(bf16[16,4,8,512]{3,0,1,2:T(8,128)(2,1)} %copy.352), calls=%async_computation | async-start | bytes 1048576 | tf_op jit(solution)/shard_map/all_to_all | solution.py:56
  17.3 6.3 %all-to-all-done = bf16[16,4,8,512]{3,0,1,2:T(8,128)(2,1)S(1)} async-done(((bf16[16,4,8,512]{3,0,1,2:T(8,128)(2,1)}), bf16[16,4,8,512]{3,0,1,2:T(8,128)(2,1)S(1)}, u32[]{:S(2)}, u32[]{:S(2)}) %all-to-all-start) | async-done | bytes 524320 | tf_op jit(solution)/shard_map/all_to_all | solution.py:56
  25.1 2.3 reduce.19
  27.4 0.9 reshape.569
  28.3 13.9 %all-to-all-start.2 = ((bf16[64,2,1024]{2,1,0:T(2,128)(2,1)}), bf16[64,2,1024]{2,1,0:T(2,128)(2,1)S(1)}, u32[]{:S(2)}, u32[]{:S(2)}) async-start(bf16[64,2,1024]{2,1,0:T(2,128)(2,1)} %reshape.569), calls=%async_computation.2 | async-start | bytes 524288 | tf_op jit(solution)/shard_map/all_to_all | solution.py:27
  44.6 7.7 %collective-permute-start = (bf16[128,4,1,512]{3,0,1,2:T(8,128)(2,1)S(1)}, bf16[128,4,1,512]{3,0,1,2:T(8,128)(2,1)S(1)}, u32[]{:S(2)}, u32[]{:S(2)}) collective-permute-start(bf16[128,4,1,512]{3,0,1,2:T(8,128)(2,1)S(1)} %bitcast.253), channel_id=1, source_target_pairs={{0,0},{2,128},{4,256},{6,384},{128,2},{130,130},{132,258},{134,386... | collective-permute-start | bytes 1572872 | tf_op jit(solution)/shard_map/ppermute | solution.py:48
  52.3 9.1 %all-to-all-done.2 = bf16[64,2,1024]{2,1,0:T(2,128)(2,1)S(1)} async-done(((bf16[64,2,1024]{2,1,0:T(2,128)(2,1)}), bf16[64,2,1024]{2,1,0:T(2,128)(2,1)S(1)}, u32[]{:S(2)}, u32[]{:S(2)}) %all-to-all-start.2) | async-done | bytes 262176 | tf_op jit(solution)/shard_map/all_to_all | solution.py:27
  62.0 3.2 collective-permute-start.3
  65.2 62.1 %collective-permute-done.3 = bf16[2048]{0:T(1024)(128)(2,1)S(1)} collective-permute-done((bf16[2048]{0:T(1024)(128)(2,1)S(1)}, bf16[2048]{0:T(1024)(128)(2,1)S(1)}, u32[]{:S(2)}, u32[]{:S(2)}) %collective-permute-start.3) | collective-permute-done | bytes 4128 | tf_op jit(solution)/shard_map/ppermute | solution.py:48
  127.6 2.3 reduce.20
  129.9 0.9 reshape.571
  130.8 7.9 %all-to-all-start.3 = ((bf16[64,2,1024]{2,1,0:T(2,128)(2,1)}), bf16[64,2,1024]{2,1,0:T(2,128)(2,1)S(1)}, u32[]{:S(2)}, u32[]{:S(2)}) async-start(bf16[64,2,1024]{2,1,0:T(2,128)(2,1)} %reshape.571), calls=%async_computation.3 | async-start | bytes 524288 | tf_op jit(solution)/shard_map/all_to_all | solution.py:34
  138.8 2.8 gather_fusion.2
  141.6 4.6 broadcast_select_fusion
  146.3 2.4 all-to-all-done.3
  148.7 8.0 %all-to-all-start.1 = ((bf16[64,32,1024]{2,1,0:T(8,128)(2,1)}), bf16[64,32,1024]{2,1,0:T(8,128)(2,1)}, u32[]{:S(2)}, u32[]{:S(2)}) async-start(bf16[64,32,1024]{2,1,0:T(8,128)(2,1)} %broadcast_select_fusion), calls=%async_computation.1 | async-start | bytes 8388608 | tf_op jit(solution)/shard_map/all_to_all | solution.py:107
  157.3 3.1 collective-permute-start.1
  160.4 7.0 %collective-permute-start.2 = (bf16[32,1024]{1,0:T(8,128)(2,1)S(1)}, bf16[32,1024]{1,0:T(8,128)(2,1)S(1)}, u32[]{:S(2)}, u32[]{:S(2)}) collective-permute-start(bf16[32,1024]{1,0:T(8,128)(2,1)S(1)} %get-tuple-element.60), channel_id=1, source_target_pairs={{8,0},{16,8},{24,16},{32,24},{40,32},{48,40},{56,48},{64,56},{72,6... | collective-permute-start | bytes 196616 | tf_op jit(solution)/shard_map/ppermute | solution.py:21
  167.5 59.3 %collective-permute-done.1 = bf16[32,1024]{1,0:T(8,128)(2,1)S(1)} collective-permute-done((bf16[32,1024]{1,0:T(8,128)(2,1)S(1)}, bf16[32,1024]{1,0:T(8,128)(2,1)S(1)}, u32[]{:S(2)}, u32[]{:S(2)}) %collective-permute-start.1) | collective-permute-done | bytes 65568 | tf_op jit(solution)/shard_map/ppermute | solution.py:20
  230.1 1.2 reshape.447
  232.5 18.1 %all-to-all-done.1 = bf16[64,32,1024]{2,1,0:T(8,128)(2,1)} async-done(((bf16[64,32,1024]{2,1,0:T(8,128)(2,1)}), bf16[64,32,1024]{2,1,0:T(8,128)(2,1)}, u32[]{:S(2)}, u32[]{:S(2)}) %all-to-all-start.1) | async-done | bytes 4194336 | tf_op jit(solution)/shard_map/all_to_all | solution.py:107
  250.7 2.8 gather_fusion.3
  253.8 1.2 slice_bitcast_fusion.1
  255.0 1.3 fusion.13
  256.3 1.2 copy.372
  259.8 1.0 convolution_bitcast_fusion.5
  261.6 1.5 reshape.448
  263.1 1.3 fusion.11
  264.4 1.2 copy.379
  265.6 1.3 reshape.445
  266.8 2.1 multiply_reduce_fusion
  271.4 25.8 %all_to_all.59 = f32[64,1,2048]{2,1,0:T(1,128)S(1)} all-to-all(f32[64,1,2048]{2,1,0:T(1,128)S(1)} %all_to_all.51), channel_id=1, replica_groups=mesh['zh'=4,'zl'=4,'y'=4,'x'=4,'core'=2] {'zl','y','x'}, dimensions={0} | all-to-all | bytes 1048576 | tf_op jit(solution)/shard_map/all_to_all | solution.py:27
  297.5 1.1 broadcast_in_dim.140
  298.6 7.2 %all-to-all-start.5 = ((f32[64,1,2048]{2,1,0:T(1,128)}), f32[64,1,2048]{2,1,0:T(1,128)S(1)}, u32[]{:S(2)}, u32[]{:S(2)}) async-start(f32[64,1,2048]{2,1,0:T(1,128)} %broadcast_in_dim.140), calls=%async_computation.5 | async-start | bytes 1048576 | tf_op jit(solution)/shard_map/all_to_all | solution.py:34
  305.9 1.3 fusion.81
  308.0 0.9 concatenate.98
  309.4 1.4 fusion.82
  311.6 0.9 concatenate.97
  312.5 1.1 pad_maximum_fusion.1
  313.6 2.5 broadcast_in_dim.142
  316.1 2.9 scatter_fusion
  319.0 2.0 all-to-all-done.5
  321.1 0.8 copy-done.5
  321.9 8.3 %all-to-all-start.6 = ((bf16[64,32,1024]{2,1,0:T(8,128)(2,1)}), bf16[64,32,1024]{2,1,0:T(8,128)(2,1)}, u32[]{:S(2)}, u32[]{:S(2)}) async-start(bf16[64,32,1024]{2,1,0:T(8,128)(2,1)} %scatter_fusion), calls=%async_computation.6 | async-start | bytes 8388608 | tf_op jit(solution)/shard_map/all_to_all | solution.py:205
  331.7 1.4 copy.448
  333.1 1.5 reshape.562
  336.3 7.8 %collective-permute-start.4 = (bf16[128,512]{1,0:T(8,128)(2,1)S(1)}, bf16[128,512]{1,0:T(8,128)(2,1)S(1)}, u32[]{:S(2)}, u32[]{:S(2)}) collective-permute-start(bf16[128,512]{1,0:T(8,128)(2,1)S(1)} %bitcast.275), channel_id=1, source_target_pairs={{0,0},{2,128},{4,256},{6,384},{128,2},{130,130},{132,258},{134,386... | collective-permute-start | bytes 393224 | tf_op jit(solution)/shard_map/ppermute | solution.py:48
  345.6 2.8 collective-permute-start.5
  348.4 7.2 %collective-permute-start.6 = (bf16[32,1024]{1,0:T(8,128)(2,1)S(1)}, bf16[32,1024]{1,0:T(8,128)(2,1)S(1)}, u32[]{:S(2)}, u32[]{:S(2)}) collective-permute-start(bf16[32,1024]{1,0:T(8,128)(2,1)S(1)} %get-tuple-element.42), channel_id=1, source_target_pairs={{8,0},{16,8},{24,16},{32,24},{40,32},{48,40},{56,48},{64,56},{72,6... | collective-permute-start | bytes 196616 | tf_op jit(solution)/shard_map/ppermute | solution.py:21
  355.9 54.6 %collective-permute-done.5 = bf16[32,1024]{1,0:T(8,128)(2,1)S(1)} collective-permute-done((bf16[32,1024]{1,0:T(8,128)(2,1)S(1)}, bf16[32,1024]{1,0:T(8,128)(2,1)S(1)}, u32[]{:S(2)}, u32[]{:S(2)}) %collective-permute-start.5) | collective-permute-done | bytes 65568 | tf_op jit(solution)/shard_map/ppermute | solution.py:20
  411.1 1.3 scatter-add.9
  412.4 1.2 reduce.16
  413.7 14.8 %all-to-all-done.6 = bf16[64,32,1024]{2,1,0:T(8,128)(2,1)} async-done(((bf16[64,32,1024]{2,1,0:T(8,128)(2,1)}), bf16[64,32,1024]{2,1,0:T(8,128)(2,1)}, u32[]{:S(2)}, u32[]{:S(2)}) %all-to-all-start.6) | async-done | bytes 4194336 | tf_op jit(solution)/shard_map/all_to_all | solution.py:205
  428.5 6.7 %fusion = f32[4,32,1024]{2,0,1:T(4,128)S(1)} fusion(bf16[64,32,1024]{2,1,0:T(8,128)(2,1)} %all-to-all-done.6, s32[64]{0:T(128)S(1)} %copy-done.24, pred[64]{0:T(512)(128)(4,1)S(1)} %gather_fusion.6), kind=kOutput, calls=%fused_computation.8 | convolution fusion | flops 16777728 | bytes 4718912 | tf_op jit(solution)/shard_map/jr,rkc->jkc/dot_general | solution.py:237
  435.2 1.0 fusion.3
  436.4 12.2 %collective-permute-start.7 = (bf16[128,512]{1,0:T(8,128)(2,1)S(1)}, bf16[128,512]{1,0:T(8,128)(2,1)S(1)}, u32[]{:S(2)}, u32[]{:S(2)}) collective-permute-start(bf16[128,512]{1,0:T(8,128)(2,1)S(1)} %bitcast.277), channel_id=1, source_target_pairs={{0,0},{2,128},{4,256},{6,384},{128,2},{130,130},{132,258},{134,386... | collective-permute-start | bytes 393224 | tf_op jit(solution)/shard_map/ppermute | solution.py:48
  448.6 1.9 collective-permute-start.8
  450.5 29.7 %collective-permute-done.7 = bf16[128,512]{1,0:T(8,128)(2,1)S(1)} collective-permute-done((bf16[128,512]{1,0:T(8,128)(2,1)S(1)}, bf16[128,512]{1,0:T(8,128)(2,1)S(1)}, u32[]{:S(2)}, u32[]{:S(2)}) %collective-permute-start.7) | collective-permute-done | bytes 131104 | tf_op jit(solution)/shard_map/ppermute | solution.py:48
  480.2 2.8 collective-permute-done.8
  (191 shorter events, 27.8 us)
Async XLA Ops:
  4.4 10.7 %copy-start.26 = (s32[4]{0:T(128)S(1)}, s32[4]{0:T(128)}, u32[]{:S(2)}) copy-start(s32[4]{0:T(128)} %param.19) | copy-start | bytes 52
  4.4 11.2 %copy-start.16 = (s32[256,3]{0,1:T(4,128)S(1)}, s32[256,3]{0,1:T(4,128)}, u32[]{:S(2)}) copy-start(s32[256,3]{0,1:T(4,128)} %param.18) | copy-start | bytes 9220
  4.5 12.1 %copy-start = (s32[64]{0:T(128)S(1)}, s32[64]{0:T(128)}, u32[]{:S(2)}) copy-start(s32[64]{0:T(128)} %constant.211.clone) | copy-start | bytes 772
  5.5 18.0 %all-to-all-start = ((bf16[16,4,8,512]{3,0,1,2:T(8,128)(2,1)}), bf16[16,4,8,512]{3,0,1,2:T(8,128)(2,1)S(1)}, u32[]{:S(2)}, u32[]{:S(2)}) async-start(bf16[16,4,8,512]{3,0,1,2:T(8,128)(2,1)} %copy.352), calls=%async_computation | async-start | bytes 1048576 | tf_op jit(solution)/shard_map/all_to_all | solution.py:56
  15.7 8.5 %copy-start.21 = (s32[4]{0:T(128)}, s32[4]{0:T(128)S(1)}, u32[]{:S(2)}) copy-start(s32[4]{0:T(128)S(1)} %get-tuple-element.62) | copy-start | bytes 52
  17.2 7.0 %copy-start.17 = (s32[12]{0:T(128)}, s32[12]{0:T(128)S(1)}, u32[]{:S(2)}) copy-start(s32[12]{0:T(128)S(1)} %fusion.78) | copy-start | bytes 148
  24.3 19.4 %copy-start.25 = (s32[64]{0:T(128)S(1)}, s32[64]{0:T(128)}, u32[]{:S(2)}) copy-start(s32[64]{0:T(128)} %constant.232) | copy-start | bytes 772
  28.3 33.1 %all-to-all-start.2 = ((bf16[64,2,1024]{2,1,0:T(2,128)(2,1)}), bf16[64,2,1024]{2,1,0:T(2,128)(2,1)S(1)}, u32[]{:S(2)}, u32[]{:S(2)}) async-start(bf16[64,2,1024]{2,1,0:T(2,128)(2,1)} %reshape.569), calls=%async_computation.2 | async-start | bytes 524288 | tf_op jit(solution)/shard_map/all_to_all | solution.py:27
  44.6 94.1 %copy-start.23 = (s32[64]{0:T(128)}, s32[64]{0:T(128)S(1)}, u32[]{:S(2)}) copy-start(s32[64]{0:T(128)S(1)} %gather_fusion.1) | copy-start | bytes 772
  44.6 94.2 %collective-permute-start = (bf16[128,4,1,512]{3,0,1,2:T(8,128)(2,1)S(1)}, bf16[128,4,1,512]{3,0,1,2:T(8,128)(2,1)S(1)}, u32[]{:S(2)}, u32[]{:S(2)}) collective-permute-start(bf16[128,4,1,512]{3,0,1,2:T(8,128)(2,1)S(1)} %bitcast.253), channel_id=1, source_target_pairs={{0,0},{2,128},{4,256},{6,384},{128,2},{130,130},{132,258},{134,386... | collective-permute-start | bytes 1572872 | tf_op jit(solution)/shard_map/ppermute | solution.py:48
  62.0 65.3 %collective-permute-start.3 = (bf16[2048]{0:T(1024)(128)(2,1)S(1)}, bf16[2048]{0:T(1024)(128)(2,1)S(1)}, u32[]{:S(2)}, u32[]{:S(2)}) collective-permute-start(bf16[2048]{0:T(1024)(128)(2,1)S(1)} %reduce_sum.71), channel_id=1, source_target_pairs={{0,0},{2,128},{4,256},{6,384},{128,2},{130,130},{132,258},{134,386... | collective-permute-start | bytes 12296 | tf_op jit(solution)/shard_map/ppermute | solution.py:48
  130.8 17.9 %all-to-all-start.3 = ((bf16[64,2,1024]{2,1,0:T(2,128)(2,1)}), bf16[64,2,1024]{2,1,0:T(2,128)(2,1)S(1)}, u32[]{:S(2)}, u32[]{:S(2)}) async-start(bf16[64,2,1024]{2,1,0:T(2,128)(2,1)} %reshape.571), calls=%async_computation.3 | async-start | bytes 524288 | tf_op jit(solution)/shard_map/all_to_all | solution.py:34
  148.7 102.0 %all-to-all-start.1 = ((bf16[64,32,1024]{2,1,0:T(8,128)(2,1)}), bf16[64,32,1024]{2,1,0:T(8,128)(2,1)}, u32[]{:S(2)}, u32[]{:S(2)}) async-start(bf16[64,32,1024]{2,1,0:T(8,128)(2,1)} %broadcast_select_fusion), calls=%async_computation.1 | async-start | bytes 8388608 | tf_op jit(solution)/shard_map/all_to_all | solution.py:107
  157.3 69.4 %collective-permute-start.1 = (bf16[32,1024]{1,0:T(8,128)(2,1)S(1)}, bf16[32,1024]{1,0:T(8,128)(2,1)S(1)}, u32[]{:S(2)}, u32[]{:S(2)}) collective-permute-start(bf16[32,1024]{1,0:T(8,128)(2,1)S(1)} %get-tuple-element.59), channel_id=1, source_target_pairs={{0,8},{8,16},{16,24},{24,32},{32,40},{40,48},{48,56},{56,64},{64,7... | collective-permute-start | bytes 196616 | tf_op jit(solution)/shard_map/ppermute | solution.py:20
  160.4 66.3 %collective-permute-start.2 = (bf16[32,1024]{1,0:T(8,128)(2,1)S(1)}, bf16[32,1024]{1,0:T(8,128)(2,1)S(1)}, u32[]{:S(2)}, u32[]{:S(2)}) collective-permute-start(bf16[32,1024]{1,0:T(8,128)(2,1)S(1)} %get-tuple-element.60), channel_id=1, source_target_pairs={{8,0},{16,8},{24,16},{32,24},{40,32},{48,40},{56,48},{64,56},{72,6... | collective-permute-start | bytes 196616 | tf_op jit(solution)/shard_map/ppermute | solution.py:21
  255.0 1.3 copy-start.2
  259.8 3.2 copy-start.4
  265.5 1.3 copy-start.15
  266.8 2.1 copy-start.9
  266.8 2.1 copy-start.12
  269.4 36.4 %copy-start.11 = (bf16[4,4,32,320]{3,2,1,0:T(8,128)(2,1)}, bf16[4,4,32,320]{3,2,1,0:T(8,128)(2,1)S(1)}, u32[]{:S(2)}) copy-start(bf16[4,4,32,320]{3,2,1,0:T(8,128)(2,1)S(1)} %fusion.18) | copy-start | bytes 983044
  269.4 1.1 copy-start.13
  297.2 8.7 %copy-start.1 = (bf16[4,4,32,6,32]{4,3,2,1,0:T(8,128)(2,1)S(1)}, bf16[4,4,32,6,32]{4,3,2,1,0:T(8,128)(2,1)}, u32[]{:S(2)}) copy-start(bf16[4,4,32,6,32]{4,3,2,1,0:T(8,128)(2,1)} %reshape.448) | copy-start | bytes 589828
  298.6 22.5 %all-to-all-start.5 = ((f32[64,1,2048]{2,1,0:T(1,128)}), f32[64,1,2048]{2,1,0:T(1,128)S(1)}, u32[]{:S(2)}, u32[]{:S(2)}) async-start(f32[64,1,2048]{2,1,0:T(1,128)} %broadcast_in_dim.140), calls=%async_computation.5 | async-start | bytes 1048576 | tf_op jit(solution)/shard_map/all_to_all | solution.py:34
  307.7 1.2 slice-start
  311.3 1.2 copy-start.10
  313.6 2.5 copy-start.18
  319.0 11.1 %copy-start.19 = (pred[256]{0:T(512)(128)(4,1)S(1)}, pred[256]{0:T(512)(128)(4,1)}, u32[]{:S(2)}) copy-start(pred[256]{0:T(512)(128)(4,1)} %get-tuple-element.29) | copy-start | bytes 772
  319.0 12.1 %copy-start.8 = (bf16[4,4,32,3,32]{4,3,2,1,0:T(4,128)(2,1)S(1)}, bf16[4,4,32,3,32]{4,3,2,1,0:T(4,128)(2,1)}, u32[]{:S(2)}) copy-start(bf16[4,4,32,3,32]{4,3,2,1,0:T(4,128)(2,1)} %get-tuple-element.37) | copy-start | bytes 294916
  321.1 0.8 copy-start.5
  321.9 106.7 %all-to-all-start.6 = ((bf16[64,32,1024]{2,1,0:T(8,128)(2,1)}), bf16[64,32,1024]{2,1,0:T(8,128)(2,1)}, u32[]{:S(2)}, u32[]{:S(2)}) async-start(bf16[64,32,1024]{2,1,0:T(8,128)(2,1)} %scatter_fusion), calls=%async_computation.6 | async-start | bytes 8388608 | tf_op jit(solution)/shard_map/all_to_all | solution.py:205
  331.7 2.9 copy-start.14
  333.1 1.8 copy-start.3
  335.0 1.0 copy-start.7
  336.3 114.2 %collective-permute-start.4 = (bf16[128,512]{1,0:T(8,128)(2,1)S(1)}, bf16[128,512]{1,0:T(8,128)(2,1)S(1)}, u32[]{:S(2)}, u32[]{:S(2)}) collective-permute-start(bf16[128,512]{1,0:T(8,128)(2,1)S(1)} %bitcast.275), channel_id=1, source_target_pairs={{0,0},{2,128},{4,256},{6,384},{128,2},{130,130},{132,258},{134,386... | collective-permute-start | bytes 393224 | tf_op jit(solution)/shard_map/ppermute | solution.py:48
  345.6 64.9 %collective-permute-start.5 = (bf16[32,1024]{1,0:T(8,128)(2,1)S(1)}, bf16[32,1024]{1,0:T(8,128)(2,1)S(1)}, u32[]{:S(2)}, u32[]{:S(2)}) collective-permute-start(bf16[32,1024]{1,0:T(8,128)(2,1)S(1)} %get-tuple-element.41), channel_id=1, source_target_pairs={{0,8},{8,16},{16,24},{24,32},{32,40},{40,48},{48,56},{56,64},{64,7... | collective-permute-start | bytes 196616 | tf_op jit(solution)/shard_map/ppermute | solution.py:20
  348.4 62.0 %collective-permute-start.6 = (bf16[32,1024]{1,0:T(8,128)(2,1)S(1)}, bf16[32,1024]{1,0:T(8,128)(2,1)S(1)}, u32[]{:S(2)}, u32[]{:S(2)}) collective-permute-start(bf16[32,1024]{1,0:T(8,128)(2,1)S(1)} %get-tuple-element.42), channel_id=1, source_target_pairs={{8,0},{16,8},{24,16},{32,24},{40,32},{48,40},{56,48},{64,56},{72,6... | collective-permute-start | bytes 196616 | tf_op jit(solution)/shard_map/ppermute | solution.py:21
  355.8 56.5 %copy-start.6 = (f32[64,1,2048]{2,1,0:T(1,128)S(1)}, f32[64,1,2048]{2,1,0:T(1,128)}, u32[]{:S(2)}) copy-start(f32[64,1,2048]{2,1,0:T(1,128)} %copy-done.5) | copy-start | bytes 1572868
  410.9 17.7 %copy-start.24 = (s32[64]{0:T(128)S(1)}, s32[64]{0:T(128)}, u32[]{:S(2)}) copy-start(s32[64]{0:T(128)} %copy-done.23) | copy-start | bytes 772
  413.7 21.5 %copy-start.20 = (pred[4]{0:T(512)(128)(4,1)S(1)}, pred[4]{0:T(512)(128)(4,1)}, u32[]{:S(2)}) copy-start(pred[4]{0:T(512)(128)(4,1)} %get-tuple-element.27) | copy-start | bytes 16
  413.7 21.5 %copy-start.22 = (s32[4]{0:T(128)S(1)}, s32[4]{0:T(128)}, u32[]{:S(2)}) copy-start(s32[4]{0:T(128)} %copy-done.21) | copy-start | bytes 52
  436.4 43.8 %collective-permute-start.7 = (bf16[128,512]{1,0:T(8,128)(2,1)S(1)}, bf16[128,512]{1,0:T(8,128)(2,1)S(1)}, u32[]{:S(2)}, u32[]{:S(2)}) collective-permute-start(bf16[128,512]{1,0:T(8,128)(2,1)S(1)} %bitcast.277), channel_id=1, source_target_pairs={{0,0},{2,128},{4,256},{6,384},{128,2},{130,130},{132,258},{134,386... | collective-permute-start | bytes 393224 | tf_op jit(solution)/shard_map/ppermute | solution.py:48
  448.6 34.4 %collective-permute-start.8 = (bf16[128,512]{1,0:T(8,128)(2,1)S(1)}, bf16[128,512]{1,0:T(8,128)(2,1)S(1)}, u32[]{:S(2)}, u32[]{:S(2)}) collective-permute-start(bf16[128,512]{1,0:T(8,128)(2,1)S(1)} %bitcast.276), channel_id=1, source_target_pairs={{0,0},{2,128},{4,256},{6,384},{128,2},{130,130},{132,258},{134,386... | collective-permute-start | bytes 393224 | tf_op jit(solution)/shard_map/ppermute | solution.py:48
